TPU v7x, 32 devices: a whole 2x2x4 slice. The times are simulated.
32 devices in a mesh: seq: 4 (over z), crow: 4 (over y, x), ccol: 2 (over core).
Axes of the slice: x: 2, y: 2, z: 4, core: 2. Of those that a mesh axis runs over, the one named last changes fastest.
Arguments:
- features: float32 [8, 768, 1024], P(None, ('crow', 'ccol'), 'seq'), may hold values from -6 to 6
- first_channel_scale: float32 [768], P(('crow', 'ccol')), may hold values from 0.5 to 2
- first_channel_shift: float32 [768], P(('crow', 'ccol')), may hold values from -3 to 3
- first_conv_bias: float32 [768], P(('crow', 'ccol')), may hold values from -3 to 3
- first_kernel_taps: float32 [5, 768, 768], P(None, ('crow', 'ccol')), may hold values from -0.09375 to 0.09375
- second_channel_scale: float32 [768], P(('crow', 'ccol')), may hold values from 0.5 to 2
- second_channel_shift: float32 [768], P(('crow', 'ccol')), may hold values from -3 to 3
- second_conv_bias: float32 [768], P(('crow', 'ccol')), may hold values from -3 to 3
- second_kernel_taps: float32 [5, 768, 768], P(None, ('crow', 'ccol')), may hold values from -0.09375 to 0.09375
- up_weight: float32 [1536, 768], P(('crow', 'ccol')), may hold values from -0.21875 to 0.21875
- norm_gain: float32 [1536], replicated, may hold values from 0.5 to 2
- qkv_weight: float32 [1536, 4608], P(None, ('crow', 'ccol')), as said below
- out_weight: float32 [1536, 1536], P(('crow', 'ccol')), may hold values from -0.625 to 0.625
Outputs:
- tower_skip_output: float32 [8, 768, 1024], P(None, ('crow', 'ccol'), 'seq')
- attended: float32 [8, 128, 1536], P(None, 'seq', ('crow', 'ccol'))
Inputs may be any that keep to these rules, and one draw needn't show every extreme that they name: `qkv_weight`: entries are of order 1 / sqrt(1536) times a few.
All inputs are finite; a program needn't handle non-finite values.
Results may differ from a plain program's by a relative error of at most 0.0003.
Values sent between devices are 32-bit elements; how exact they have to be, the bound alone decides.
No kernel may reach another device: no remote copies, remote signals or barrier semaphores. Data moves between devices by JAX's collectives and lax.ppermute only.
A program may use at most 192 MiB of HBM per device.

v0:
```python
import math

import jax
import jax.numpy as jnp
from jax import lax
from jax.sharding import PartitionSpec as P

FIRST_DILATION = 2
SECOND_DILATION = 4
POOL = 8
TAPS = 5

MATMUL_PRECISION = lax.Precision.HIGH
CHANNELS = ("crow", "ccol")


def gathered(x, axis_name):
    count = lax.axis_size(axis_name)
    copies = jnp.broadcast_to(x[None], (count,) + x.shape)
    return lax.all_to_all(copies, axis_name, 0, 0, tiled=True)


def summed_scatter(x, axis_name):
    return jnp.sum(lax.all_to_all(x, axis_name, 0, 0, tiled=True), axis=0)


def swap_ccol(x):
    return lax.ppermute(x, "ccol", [(0, 1), (1, 0)])


def shifted_in(edge, forward):
    count = lax.axis_size("seq")
    if forward:
        pairs = [(i, i + 1) for i in range(count - 1)]
    else:
        pairs = [(i + 1, i) for i in range(count - 1)]
    return lax.ppermute(edge, "seq", pairs)


def convolution_block(inputs, bn_scale, bn_shift, conv_bias, kernel, dilation):
    activated = jax.nn.gelu(inputs * bn_scale[:, None] + bn_shift[:, None], approximate=False)
    by_row = gathered(activated, "crow")
    other_core = swap_ccol(by_row)
    core = lax.axis_index("ccol")
    tap_count, out_count, in_count = kernel.shape
    row_count = lax.axis_size("crow")
    block = in_count // (2 * row_count)
    weights = jnp.transpose(kernel.reshape(tap_count * out_count, in_count))
    weights = weights.reshape(row_count, 2, block, tap_count * out_count)
    own_weights = lax.dynamic_index_in_dim(weights, core, axis=1, keepdims=False)
    other_weights = lax.dynamic_index_in_dim(weights, 1 - core, axis=1, keepdims=False)
    products = jnp.einsum(
        "rbit,rio->bot", by_row, own_weights, precision=MATMUL_PRECISION
    ) + jnp.einsum("rbit,rio->bot", other_core, other_weights, precision=MATMUL_PRECISION)
    batch_count, rows = inputs.shape[0], inputs.shape[2]
    products = products.reshape(batch_count, tap_count, out_count, rows)
    width = 2 * dilation
    padded = jnp.pad(products, ((0, 0), (0, 0), (0, 0), (2 * width, 2 * width)))
    spread = None
    for tap_index in range(tap_count):
        offset = tap_index * dilation
        term = padded[:, tap_index, :, offset : offset + rows + 2 * width]
        spread = term if spread is None else spread + term
    to_left = jnp.swapaxes(spread[..., :width], 1, 2)
    to_right = jnp.swapaxes(spread[..., rows + width :], 1, 2)
    from_left = jnp.swapaxes(shifted_in(to_right, True), 1, 2)
    from_right = jnp.swapaxes(shifted_in(to_left, False), 1, 2)
    edges = jnp.concatenate(
        [from_left, jnp.zeros((batch_count, out_count, rows - 2 * width), jnp.float32), from_right],
        axis=2,
    )
    summed = spread[..., width : width + rows] + edges
    return inputs + summed + conv_bias[:, None]


def rotate(values, positions):
    half_width = values.shape[-1] // 2
    frequency = jnp.exp(
        -math.log(10000.0) * jnp.arange(half_width).astype(jnp.float32) / half_width
    )
    angle = positions[:, None] * frequency[None, :]
    cosine = jnp.cos(angle)
    sine_part = jnp.sin(angle)
    lower_half = values[..., :half_width]
    upper_half = values[..., half_width:]
    return jnp.concatenate(
        [
            lower_half * cosine - upper_half * sine_part,
            lower_half * sine_part + upper_half * cosine,
        ],
        axis=-1,
    )


def per_device(
    features,
    first_channel_scale,
    first_channel_shift,
    first_conv_bias,
    first_kernel_taps,
    second_channel_scale,
    second_channel_shift,
    second_conv_bias,
    second_kernel_taps,
    up_weight,
    norm_gain,
    qkv_weight,
    out_weight,
):
    batch_count = features.shape[0]
    channels = features.shape[1]
    row_count = features.shape[2]
    first_part = convolution_block(
        features,
        first_channel_scale,
        first_channel_shift,
        first_conv_bias,
        first_kernel_taps,
        FIRST_DILATION,
    )
    tower_skip_output = convolution_block(
        first_part,
        second_channel_scale,
        second_channel_shift,
        second_conv_bias,
        second_kernel_taps,
        SECOND_DILATION,
    )
    pooled_rows = row_count // POOL
    pooled = jnp.transpose(
        jnp.max(tower_skip_output.reshape(batch_count, channels, pooled_rows, POOL), axis=3),
        (0, 2, 1),
    )
    group = lax.axis_size(CHANNELS)
    pooled_all = gathered(pooled, CHANNELS)
    up_blocks = up_weight.reshape(up_weight.shape[0], group, channels)
    hidden = jnp.einsum("nbti,oni->bto", pooled_all, up_blocks, precision=MATMUL_PRECISION)
    hidden_all = gathered(hidden, CHANNELS)
    attn_width = norm_gain.shape[0]
    squares = jnp.sum(hidden_all * hidden_all, axis=(0, 3))
    gain_blocks = norm_gain.reshape(group, 1, 1, attn_width // group)
    qkv_blocks = qkv_weight.reshape(group, attn_width // group, qkv_weight.shape[1])
    projected = jnp.einsum(
        "nbtj,njo->bto", hidden_all * gain_blocks, qkv_blocks, precision=MATMUL_PRECISION
    )
    root_mean = jnp.sqrt(squares / attn_width + 1e-06)
    projected = projected / root_mean[..., None]
    head_extent = qkv_weight.shape[1] // 3
    positions = (
        lax.axis_index("seq") * pooled_rows + jnp.arange(pooled_rows, dtype=jnp.int32)
    ).astype(jnp.float32)
    query_rows = rotate(projected[..., :head_extent], positions) / math.sqrt(head_extent)
    key_matrix = rotate(projected[..., head_extent : 2 * head_extent], positions)
    keys_and_values = jnp.concatenate([key_matrix, projected[..., 2 * head_extent :]], axis=2)
    kv_all = gathered(keys_and_values, "seq")
    attention_scores = jnp.einsum(
        "btc,nbxc->btnx", query_rows, kv_all[..., :head_extent], precision=MATMUL_PRECISION
    )
    top = jnp.max(attention_scores, axis=(2, 3))
    probabilities = jnp.exp(attention_scores - top[..., None, None])
    denominator = jnp.sum(probabilities, axis=(2, 3))
    weighted_values = jnp.einsum(
        "btnx,nbxe->bte", probabilities, kv_all[..., head_extent:], precision=MATMUL_PRECISION
    )
    head_result = weighted_values / denominator[..., None]
    out_blocks = out_weight.reshape(out_weight.shape[0], group, out_weight.shape[1] // group)
    shares = jnp.einsum("btd,dne->nbte", head_result, out_blocks, precision=MATMUL_PRECISION)
    attended = summed_scatter(shares, CHANNELS)
    return (tower_skip_output, attended)


def solution(mesh):
    placed = (
        P(None, CHANNELS, "seq"),
        P(CHANNELS),
        P(CHANNELS),
        P(CHANNELS),
        P(None, CHANNELS, None),
        P(CHANNELS),
        P(CHANNELS),
        P(CHANNELS),
        P(None, CHANNELS, None),
        P(CHANNELS, None),
        P(),
        P(None, CHANNELS),
        P(CHANNELS, None),
    )
    return jax.shard_map(
        per_device,
        mesh=mesh,
        in_specs=placed,
        out_specs=(P(None, CHANNELS, "seq"), P(None, "seq", CHANNELS)),
        check_vma=False,
    )
```

profile of v0, /device:TPU:0, one launch (start us, length us, event | category | flops | bytes accessed | tf_op | source)
XLA Modules:
  0.0 295.5 jit_solution(1305220644913792253)
XLA Ops:
  2.1 3.0 %fusion.23 = f32[8,96,256]{1,2,0:T(8,128)S(1)} fusion(f32[8,96,256]{1,2,0:T(8,128)S(1)} %copy.51, f32[96]{0:T(128)} %param.15, f32[96]{0:T(128)} %param.14), kind=kLoop, calls=%fused_computation.37 | loop fusion | flops 12976128 | bytes 1573632 | tf_op jit(solution)/shard_map/mul | solution.py:41
  5.8 41.6 %all_to_all.30 = f32[4,8,96,256]{3,2,1,0:T(8,128)S(1)} all-to-all(f32[4,8,96,256]{3,2,1,0:T(8,128)S(1)} %broadcast_in_dim.14), channel_id=1, replica_groups=mesh['seq'=4,'crow'=4,'ccol'=2] {'crow'}, dimensions={0} | all-to-all | bytes 6291456 | tf_op jit(solution)/shard_map/all_to_all | solution.py:20
  47.4 1.9 copy.48
  49.3 3.0 %copy.45 = f32[768,480]{1,0:T(8,128)} copy(f32[768,480]{0,1:T(8,128)} %bitcast.119) | data formatting | bytes 2949120 | tf_op jit(solution)/shard_map/transpose | solution.py:48
  52.3 4.8 %fusion.50 = f32[480,8,256,1]{2,0,1,3:T(8,128)S(1)} fusion(f32[4,8,96,256]{3,2,1,0:T(8,128)S(1)} %all_to_all.30, f32[4,2,96,480]{3,2,1,0:T(8,128)} %bitcast.114, s32[]{:T(128)S(6)} %select_n.9), kind=kOutput, calls=%fused_computation.85 | convolution fusion | flops 2264924160 | bytes 7864324 | tf_op jit(solution)/shard_map/rbit,rio->bot/dot_general | solution.py:52
  57.1 7.4 %bitcast_add_fusion.1 = f32[480,8,256]{2,0,1:T(8,128)} fusion(f32[480,8,256,1]{2,0,1,3:T(8,128)S(1)} %fusion.50, f32[4,8,96,256]{3,2,0,1:T(8,128)} %collective-permute-done, f32[4,2,96,480]{3,2,1,0:T(8,128)S(1)} %bitcast.115, s32[]{:T(128)S(6)} %select_n.10), kind=kOutput, calls=%fused_computation.11 | convolution fusion | flops 2265907200 | bytes 11796484 | tf_op jit(solution)/shard_map/rbit,rio->bot/dot_general | solution.py:54
  64.4 5.6 %copy.50 = f32[8,5,96,256]{2,3,0,1:T(8,128)} copy(f32[8,5,96,256]{3,2,1,0:T(8,128)} %bitcast.112) | data formatting | bytes 7864320 | tf_op jit(solution)/shard_map/reshape | solution.py:56
  70.0 3.1 %fusion.21 = f32[8,96,264]{1,2,0:T(8,128)S(1)} fusion(f32[8,5,96,256]{2,3,0,1:T(8,128)} %copy.50), kind=kLoop, calls=%fused_computation.35 | loop fusion | flops 811008 | bytes 4743168 | tf_op jit(solution)/shard_map/add | solution.py:63
  73.2 3.5 %collective-permute-start.1 = (f32[8,4,96]{2,1,0:T(4,128)S(1)}, f32[8,4,96]{2,1,0:T(4,128)S(1)}, u32[]{:S(2)}, u32[]{:S(2)}) collective-permute-start(f32[8,4,96]{2,1,0:T(4,128)S(1)} %get-tuple-element.14), channel_id=1, source_target_pairs={{0,8},{8,16},{16,24},{1,9},{9,17},{17,25},{2,10},{10,18},{18,26},{... | collective-permute-start | bytes 36872 | tf_op jit(solution)/shard_map/ppermute | solution.py:37
  78.2 4.1 %collective-permute-done.2 = f32[8,4,96]{2,1,0:T(4,128)S(1)} collective-permute-done((f32[8,4,96]{2,1,0:T(4,128)S(1)}, f32[8,4,96]{2,1,0:T(4,128)S(1)}, u32[]{:S(2)}, u32[]{:S(2)}) %collective-permute-start.2) | collective-permute-done | bytes 12320 | tf_op jit(solution)/shard_map/ppermute | solution.py:37
  82.3 2.9 fusion.25
  85.9 38.6 %all_to_all.31 = f32[4,8,96,256]{3,2,1,0:T(8,128)S(1)} all-to-all(f32[4,8,96,256]{3,2,1,0:T(8,128)S(1)} %broadcast_in_dim.16), channel_id=1, replica_groups=mesh['seq'=4,'crow'=4,'ccol'=2] {'crow'}, dimensions={0} | all-to-all | bytes 6291456 | tf_op jit(solution)/shard_map/all_to_all | solution.py:20
  124.5 1.9 copy.54
  126.5 3.0 %copy.52 = f32[768,480]{1,0:T(8,128)} copy(f32[768,480]{0,1:T(8,128)} %bitcast.120) | data formatting | bytes 2949120 | tf_op jit(solution)/shard_map/transpose | solution.py:48
  129.5 4.8 %fusion.48 = f32[480,8,256,1]{2,0,1,3:T(8,128)S(1)} fusion(f32[4,8,96,256]{3,2,1,0:T(8,128)S(1)} %all_to_all.31, f32[4,2,96,480]{3,2,1,0:T(8,128)} %bitcast.116, s32[]{:T(128)S(6)} %select_n.9), kind=kOutput, calls=%fused_computation.83 | convolution fusion | flops 2264924160 | bytes 7864324 | tf_op jit(solution)/shard_map/rbit,rio->bot/dot_general | solution.py:52
  134.3 7.3 %bitcast_add_fusion = f32[480,8,256]{2,0,1:T(8,128)} fusion(f32[480,8,256,1]{2,0,1,3:T(8,128)S(1)} %fusion.48, f32[4,8,96,256]{3,2,0,1:T(8,128)} %collective-permute-done.3, f32[4,2,96,480]{3,2,1,0:T(8,128)S(1)} %bitcast.117, s32[]{:T(128)S(6)} %select_n.10), kind=kOutput, calls=%fused_computation.10 | convolution fusion | flops 2265907200 | bytes 11796484 | tf_op jit(solution)/shard_map/rbit,rio->bot/dot_general | solution.py:54
  141.6 5.6 %copy.56 = f32[8,5,96,256]{2,3,0,1:T(8,128)} copy(f32[8,5,96,256]{3,2,1,0:T(8,128)} %bitcast.111) | data formatting | bytes 7864320 | tf_op jit(solution)/shard_map/reshape | solution.py:56
  147.2 3.1 %fusion.14 = f32[8,96,272]{1,2,0:T(8,128)S(1)} fusion(f32[8,5,96,256]{2,3,0,1:T(8,128)} %copy.56), kind=kLoop, calls=%fused_computation.28 | loop fusion | flops 835584 | bytes 4767744 | tf_op jit(solution)/shard_map/add | solution.py:63
  150.3 3.5 %collective-permute-start.4 = (f32[8,8,96]{2,1,0:T(8,128)S(1)}, f32[8,8,96]{2,1,0:T(8,128)S(1)}, u32[]{:S(2)}, u32[]{:S(2)}) collective-permute-start(f32[8,8,96]{2,1,0:T(8,128)S(1)} %get-tuple-element.12), channel_id=1, source_target_pairs={{0,8},{8,16},{16,24},{1,9},{9,17},{17,25},{2,10},{10,18},{18,26},{... | collective-permute-start | bytes 73736 | tf_op jit(solution)/shard_map/ppermute | solution.py:37
  155.4 4.2 %collective-permute-done.5 = f32[8,8,96]{2,1,0:T(8,128)S(1)} collective-permute-done((f32[8,8,96]{2,1,0:T(8,128)S(1)}, f32[8,8,96]{2,1,0:T(8,128)S(1)}, u32[]{:S(2)}, u32[]{:S(2)}) %collective-permute-start.5) | collective-permute-done | bytes 24608 | tf_op jit(solution)/shard_map/ppermute | solution.py:37
  159.6 1.7 bitcast_reduce_fusion
  162.4 3.8 %all-to-all-start.2 = ((f32[8,8,32,96]{3,2,1,0:T(8,128)}), f32[8,8,32,96]{3,2,1,0:T(8,128)S(1)}, u32[]{:S(2)}, u32[]{:S(2)}) async-start(f32[8,8,32,96]{3,2,1,0:T(8,128)} %broadcast_in_dim.18), calls=%async_computation.2 | async-start | bytes 2097152 | tf_op jit(solution)/shard_map/all_to_all | solution.py:20
  166.6 14.7 %all-to-all-done.2 = f32[8,8,32,96]{3,2,1,0:T(8,128)S(1)} async-done(((f32[8,8,32,96]{3,2,1,0:T(8,128)}), f32[8,8,32,96]{3,2,1,0:T(8,128)S(1)}, u32[]{:S(2)}, u32[]{:S(2)}) %all-to-all-start.2) | async-done | bytes 786464 | tf_op jit(solution)/shard_map/all_to_all | solution.py:20
  183.6 3.6 %all-to-all-start.3 = ((f32[8,8,32,192]{3,2,1,0:T(8,128)}), f32[8,8,32,192]{3,2,1,0:T(8,128)S(1)}, u32[]{:S(2)}, u32[]{:S(2)}) async-start(f32[8,8,32,192]{3,2,1,0:T(8,128)} %broadcast_in_dim.19), calls=%async_computation.3 | async-start | bytes 4194304 | tf_op jit(solution)/shard_map/all_to_all | solution.py:20
  187.3 5.3 %copy.59 = f32[1536,576]{1,0:T(8,128)} copy(f32[1536,576]{0,1:T(8,128)} %param.24) | data formatting | bytes 7077888 | tf_op args[11]
  192.8 21.0 %all-to-all-done.3 = f32[8,8,32,192]{3,2,1,0:T(8,128)S(1)} async-done(((f32[8,8,32,192]{3,2,1,0:T(8,128)}), f32[8,8,32,192]{3,2,1,0:T(8,128)S(1)}, u32[]{:S(2)}, u32[]{:S(2)}) %all-to-all-start.3) | async-done | bytes 1572896 | tf_op jit(solution)/shard_map/all_to_all | solution.py:20
  214.1 4.5 %fusion.7 = f32[8,32,576]{2,1,0:T(8,128)S(1)} fusion(f32[8,192,576,1]{2,1,3,0:T(8,128)} %bitcast.113, f32[8,8,32,192]{3,2,1,0:T(8,128)S(1)} %all-to-all-done.3, f32[8,192]{1,0:T(8,128)S(1)} %mul.142, f32[8,32]{1,0:T(8,128)S(1)} %add_sqrt_fusion), kind=kOutput, calls=%fused_computation.21 | convolution fusion | flops 1359495168 | bytes 5708800 | tf_op jit(solution)/shard_map/nbtj,njo->bto/dot_general | solution.py:143
  220.3 3.6 %all-to-all-start.4 = ((f32[4,8,32,384]{3,2,1,0:T(8,128)}), f32[4,8,32,384]{3,2,1,0:T(8,128)S(1)}, u32[]{:S(2)}, u32[]{:S(2)}) async-start(f32[4,8,32,384]{3,2,1,0:T(8,128)} %broadcast_in_dim.20), calls=%async_computation.4 | async-start | bytes 3145728 | tf_op jit(solution)/shard_map/all_to_all | solution.py:20
  223.9 1.7 reshape.137
  225.6 32.6 %all-to-all-done.4 = f32[4,8,32,384]{3,2,1,0:T(8,128)S(1)} async-done(((f32[4,8,32,384]{3,2,1,0:T(8,128)}), f32[4,8,32,384]{3,2,1,0:T(8,128)S(1)}, u32[]{:S(2)}, u32[]{:S(2)}) %all-to-all-start.4) | async-done | bytes 1572896 | tf_op jit(solution)/shard_map/all_to_all | solution.py:20
  263.0 5.0 %all-to-all-start.5 = ((f32[8,8,32,192]{3,2,1,0:T(8,128)}), f32[8,8,32,192]{3,2,1,0:T(8,128)S(1)}, u32[]{:S(2)}, u32[]{:S(2)}) async-start(f32[8,8,32,192]{3,2,1,0:T(8,128)} %copy.65), calls=%async_computation.5 | async-start | bytes 4194304 | tf_op jit(solution)/shard_map/all_to_all | solution.py:24
  269.2 25.4 %all-to-all-done.5 = f32[8,8,32,192]{3,2,1,0:T(8,128)S(1)} async-done(((f32[8,8,32,192]{3,2,1,0:T(8,128)}), f32[8,8,32,192]{3,2,1,0:T(8,128)S(1)}, u32[]{:S(2)}, u32[]{:S(2)}) %all-to-all-start.5) | async-done | bytes 1572896 | tf_op jit(solution)/shard_map/all_to_all | solution.py:24
  (69 shorter events, 18.9 us)
Async XLA Ops:
  2.1 3.3 %copy-start = (f32[8,96,256]{1,2,0:T(8,128)}, f32[8,96,256]{1,2,0:T(8,128)S(1)}, u32[]{:S(2)}) copy-start(f32[8,96,256]{1,2,0:T(8,128)S(1)} %copy.51) | copy-start | bytes 2359300
  49.3 7.8 %collective-permute-start = (f32[4,8,96,256]{3,2,0,1:T(8,128)}, f32[4,8,96,256]{3,2,0,1:T(8,128)}, u32[]{:S(2)}, u32[]{:S(2)}) collective-permute-start(f32[4,8,96,256]{3,2,0,1:T(8,128)} %copy.48), channel_id=1, source_target_pairs={{0,1},{1,0},{2,3},{3,2},{4,5},{5,4},{6,7},{7,6},{8,9},{9,8},{10,11... | collective-permute-start | bytes 9437192 | tf_op jit(solution)/shard_map/ppermute | solution.py:28
  52.3 4.8 %copy-start.5 = (f32[768,480]{1,0:T(8,128)S(1)}, f32[768,480]{1,0:T(8,128)}, u32[]{:S(2)}) copy-start(f32[768,480]{1,0:T(8,128)} %copy.45) | copy-start | bytes 4423684
  70.0 12.3 %copy-start.1 = (f32[8,96,256]{1,2,0:T(8,128)S(1)}, f32[8,96,256]{1,2,0:T(8,128)}, u32[]{:S(2)}) copy-start(f32[8,96,256]{1,2,0:T(8,128)} %copy-done) | copy-start | bytes 2359300
  70.0 12.3 %copy-start.10 = (f32[96]{0:T(128)S(1)}, f32[96]{0:T(128)}, u32[]{:S(2)}) copy-start(f32[96]{0:T(128)} %param.16) | copy-start | bytes 1156
  70.0 12.3 %copy-start.11 = (f32[96]{0:T(128)S(1)}, f32[96]{0:T(128)}, u32[]{:S(2)}) copy-start(f32[96]{0:T(128)} %param.19) | copy-start | bytes 1156
  70.0 12.3 %copy-start.12 = (f32[96]{0:T(128)S(1)}, f32[96]{0:T(128)}, u32[]{:S(2)}) copy-start(f32[96]{0:T(128)} %param.18) | copy-start | bytes 1156
  73.1 9.2 %copy-start.3 = (f32[8,96,264]{1,2,0:T(8,128)}, f32[8,96,264]{1,2,0:T(8,128)S(1)}, u32[]{:S(2)}) copy-start(f32[8,96,264]{1,2,0:T(8,128)S(1)} %fusion.21) | copy-start | bytes 2433028
  73.2 5.1 %collective-permute-start.1 = (f32[8,4,96]{2,1,0:T(4,128)S(1)}, f32[8,4,96]{2,1,0:T(4,128)S(1)}, u32[]{:S(2)}, u32[]{:S(2)}) collective-permute-start(f32[8,4,96]{2,1,0:T(4,128)S(1)} %get-tuple-element.14), channel_id=1, source_target_pairs={{0,8},{8,16},{16,24},{1,9},{9,17},{17,25},{2,10},{10,18},{18,26},{... | collective-permute-start | bytes 36872 | tf_op jit(solution)/shard_map/ppermute | solution.py:37
  76.7 5.6 %collective-permute-start.2 = (f32[8,4,96]{2,1,0:T(4,128)S(1)}, f32[8,4,96]{2,1,0:T(4,128)S(1)}, u32[]{:S(2)}, u32[]{:S(2)}) collective-permute-start(f32[8,4,96]{2,1,0:T(4,128)S(1)} %get-tuple-element.15), channel_id=1, source_target_pairs={{8,0},{16,8},{24,16},{9,1},{17,9},{25,17},{10,2},{18,10},{26,18},{... | collective-permute-start | bytes 36872 | tf_op jit(solution)/shard_map/ppermute | solution.py:37
  126.5 7.8 %collective-permute-start.3 = (f32[4,8,96,256]{3,2,0,1:T(8,128)}, f32[4,8,96,256]{3,2,0,1:T(8,128)}, u32[]{:S(2)}, u32[]{:S(2)}) collective-permute-start(f32[4,8,96,256]{3,2,0,1:T(8,128)} %copy.54), channel_id=1, source_target_pairs={{0,1},{1,0},{2,3},{3,2},{4,5},{5,4},{6,7},{7,6},{8,9},{9,8},{10,11... | collective-permute-start | bytes 9437192 | tf_op jit(solution)/shard_map/ppermute | solution.py:28
  129.5 4.8 %copy-start.6 = (f32[768,480]{1,0:T(8,128)S(1)}, f32[768,480]{1,0:T(8,128)}, u32[]{:S(2)}) copy-start(f32[768,480]{1,0:T(8,128)} %copy.52) | copy-start | bytes 4423684
  147.2 12.4 %copy-start.2 = (f32[8,96,256]{1,2,0:T(8,128)S(1)}, f32[8,96,256]{1,2,0:T(8,128)}, u32[]{:S(2)}) copy-start(f32[8,96,256]{1,2,0:T(8,128)} %copy-done) | copy-start | bytes 2359300
  147.2 12.4 %copy-start.4 = (f32[8,96,264]{1,2,0:T(8,128)S(1)}, f32[8,96,264]{1,2,0:T(8,128)}, u32[]{:S(2)}) copy-start(f32[8,96,264]{1,2,0:T(8,128)} %copy-done.3) | copy-start | bytes 2433028
  147.2 12.4 %copy-start.13 = (f32[96]{0:T(128)S(1)}, f32[96]{0:T(128)}, u32[]{:S(2)}) copy-start(f32[96]{0:T(128)} %param.20) | copy-start | bytes 1156
  150.3 5.1 %collective-permute-start.4 = (f32[8,8,96]{2,1,0:T(8,128)S(1)}, f32[8,8,96]{2,1,0:T(8,128)S(1)}, u32[]{:S(2)}, u32[]{:S(2)}) collective-permute-start(f32[8,8,96]{2,1,0:T(8,128)S(1)} %get-tuple-element.12), channel_id=1, source_target_pairs={{0,8},{8,16},{16,24},{1,9},{9,17},{17,25},{2,10},{10,18},{18,26},{... | collective-permute-start | bytes 73736 | tf_op jit(solution)/shard_map/ppermute | solution.py:37
  153.8 5.8 %collective-permute-start.5 = (f32[8,8,96]{2,1,0:T(8,128)S(1)}, f32[8,8,96]{2,1,0:T(8,128)S(1)}, u32[]{:S(2)}, u32[]{:S(2)}) collective-permute-start(f32[8,8,96]{2,1,0:T(8,128)S(1)} %get-tuple-element.13), channel_id=1, source_target_pairs={{8,0},{16,8},{24,16},{9,1},{17,9},{25,17},{10,2},{18,10},{26,18},{... | collective-permute-start | bytes 73736 | tf_op jit(solution)/shard_map/ppermute | solution.py:37
  161.3 4.9 %copy-start.8 = (f32[192,768]{1,0:T(8,128)S(1)}, f32[192,768]{1,0:T(8,128)}, u32[]{:S(2)}) copy-start(f32[192,768]{1,0:T(8,128)} %param.22) | copy-start | bytes 1769476
  162.4 18.9 %all-to-all-start.2 = ((f32[8,8,32,96]{3,2,1,0:T(8,128)}), f32[8,8,32,96]{3,2,1,0:T(8,128)S(1)}, u32[]{:S(2)}, u32[]{:S(2)}) async-start(f32[8,8,32,96]{3,2,1,0:T(8,128)} %broadcast_in_dim.18), calls=%async_computation.2 | async-start | bytes 2097152 | tf_op jit(solution)/shard_map/all_to_all | solution.py:20
  183.6 30.2 %all-to-all-start.3 = ((f32[8,8,32,192]{3,2,1,0:T(8,128)}), f32[8,8,32,192]{3,2,1,0:T(8,128)S(1)}, u32[]{:S(2)}, u32[]{:S(2)}) async-start(f32[8,8,32,192]{3,2,1,0:T(8,128)} %broadcast_in_dim.19), calls=%async_computation.3 | async-start | bytes 4194304 | tf_op jit(solution)/shard_map/all_to_all | solution.py:20
  187.3 5.3 %copy-start.9 = (f32[1536]{0:T(1024)S(1)}, f32[1536]{0:T(1024)}, u32[]{:S(2)}) copy-start(f32[1536]{0:T(1024)} %param.23) | copy-start | bytes 18436
  220.3 37.9 %all-to-all-start.4 = ((f32[4,8,32,384]{3,2,1,0:T(8,128)}), f32[4,8,32,384]{3,2,1,0:T(8,128)S(1)}, u32[]{:S(2)}, u32[]{:S(2)}) async-start(f32[4,8,32,384]{3,2,1,0:T(8,128)} %broadcast_in_dim.20), calls=%async_computation.4 | async-start | bytes 3145728 | tf_op jit(solution)/shard_map/all_to_all | solution.py:20
  263.0 5.0 %copy-start.7 = (f32[8,96,256]{1,2,0:T(8,128)S(1)}, f32[8,96,256]{1,2,0:T(8,128)}, u32[]{:S(2)}) copy-start(f32[8,96,256]{1,2,0:T(8,128)} %get-tuple-element.9) | copy-start | bytes 2359300
  263.0 31.7 %all-to-all-start.5 = ((f32[8,8,32,192]{3,2,1,0:T(8,128)}), f32[8,8,32,192]{3,2,1,0:T(8,128)S(1)}, u32[]{:S(2)}, u32[]{:S(2)}) async-start(f32[8,8,32,192]{3,2,1,0:T(8,128)} %copy.65), calls=%async_computation.5 | async-start | bytes 4194304 | tf_op jit(solution)/shard_map/all_to_all | solution.py:24
where the time goes:
time: 297 us; the launch traced here: 296 us
  waiting for transfers between devices  102 us (34%)
  blocking collectives  80.2 us (27%)
  local copies, waits for them, and re-layouts  38.7 us (13%)
  matrix products  32.2 us (11%)
  starting transfers between devices  25.7 us (9%)
  other arithmetic  15.5 us (5%)
    all_to_all x2, blocking collectives, gathered(): return lax.all_to_all(copies, axis_name, 0, 0, tiled=True)  80.2 us
    all_to_all x3, waiting for transfers between devices, gathered(): return lax.all_to_all(copies, axis_name, 0, 0, tiled=True)  68.4 us
    all_to_all x1, waiting for transfers between devices, summed_scatter(): return jnp.sum(lax.all_to_all(x, axis_name, 0, 0, tiled=True), axis=0)  25.4 us
    dot_general x2, matrix products, convolution_block(): jnp.einsum('rbit,rio->bot', other_core, other_weights, precision=MATMUL_P...  14.7 us
    reshape x2, local copies, waits for them, and re-layouts, convolution_block(): products = products.reshape(batch_count, tap_count, out_count, rows)  11.2 us
    all_to_all x3, starting transfers between devices, gathered(): return lax.all_to_all(copies, axis_name, 0, 0, tiled=True)  10.9 us
    ppermute x4, starting transfers between devices, shifted_in(): return lax.ppermute(edge, 'seq', pairs)  9.73 us
    dot_general x2, matrix products, convolution_block(): jnp.einsum('rbit,rio->bot', by_row, own_weights, precision=MATMUL_PRECISION)  9.51 us
  transfers between devices with their start and end apart: 10, of which 7 were waited for; matrix products, arithmetic and copies ran while one was open for 8% of the time, Pallas kernels for 0%

commit v1 on v0

--- a/solution.py
+++ b/solution.py
@@ -92,6 +92,107 @@
     )
 
 
+LANES = 128
+
+
+def packed(x):
+    rows, width = x.shape[-2:]
+    if (rows * width) % LANES:
+        return x
+    return x.reshape(x.shape[:-2] + (rows * width // LANES, LANES))
+
+
+def unpacked(x, rows, width):
+    return x.reshape(x.shape[:-2] + (rows, width))
+
+
+def gathered_packed(x, axis_name):
+    rows, width = x.shape[-2:]
+    return unpacked(gathered(packed(x), axis_name), rows, width)
+
+
+def head_attention(hidden_all, norm_gain, qkv_weight, positions):
+    group = hidden_all.shape[0]
+    attn_width = norm_gain.shape[0]
+    squares = jnp.sum(hidden_all * hidden_all, axis=(0, 3))
+    gain_blocks = norm_gain.reshape(group, 1, 1, attn_width // group)
+    qkv_blocks = qkv_weight.reshape(group, attn_width // group, qkv_weight.shape[1])
+    projected = jnp.einsum(
+        "nbtj,njo->bto", hidden_all * gain_blocks, qkv_blocks, precision=MATMUL_PRECISION
+    )
+    root_mean = jnp.sqrt(squares / attn_width + 1e-06)
+    projected = projected / root_mean[..., None]
+    head_extent = qkv_weight.shape[1] // 3
+    query_rows = rotate(projected[..., :head_extent], positions) / math.sqrt(head_extent)
+    key_matrix = rotate(projected[..., head_extent : 2 * head_extent], positions)
+    return query_rows, key_matrix, projected[..., 2 * head_extent :]
+
+
+def attention_by_batch(pooled, up_weight, norm_gain, qkv_weight, out_weight):
+    batch_count, pooled_rows, channels = pooled.shape
+    seq = lax.axis_size("seq")
+    group = lax.axis_size(CHANNELS)
+    per = batch_count // seq
+    length = seq * pooled_rows
+    mine = lax.all_to_all(pooled.reshape(seq, per, pooled_rows, channels), "seq", 0, 0, tiled=True)
+    mine = jnp.transpose(mine, (1, 0, 2, 3)).reshape(per, length, channels)
+    pooled_all = gathered_packed(mine, CHANNELS)
+    up_blocks = up_weight.reshape(up_weight.shape[0], group, channels)
+    hidden = jnp.einsum("nbti,oni->bto", pooled_all, up_blocks, precision=MATMUL_PRECISION)
+    hidden_all = gathered_packed(hidden, CHANNELS)
+    positions = jnp.arange(length, dtype=jnp.int32).astype(jnp.float32)
+    query_rows, key_matrix, value_matrix = head_attention(hidden_all, norm_gain, qkv_weight, positions)
+    attention_scores = jnp.einsum(
+        "btc,bxc->btx", query_rows, key_matrix, precision=MATMUL_PRECISION
+    )
+    top = jnp.max(attention_scores, axis=2)
+    probabilities = jnp.exp(attention_scores - top[..., None])
+    denominator = jnp.sum(probabilities, axis=2)
+    weighted_values = jnp.einsum(
+        "btx,bxe->bte", probabilities, value_matrix, precision=MATMUL_PRECISION
+    )
+    head_result = weighted_values / denominator[..., None]
+    out_width = out_weight.shape[1] // group
+    out_blocks = out_weight.reshape(out_weight.shape[0], group, out_width)
+    shares = jnp.einsum("btd,dne->nbte", head_result, out_blocks, precision=MATMUL_PRECISION)
+    summed = jnp.sum(lax.all_to_all(packed(shares), CHANNELS, 0, 0, tiled=True), axis=0)
+    summed = unpacked(summed, length, out_width)
+    by_block = jnp.transpose(summed.reshape(per, seq, pooled_rows, out_width), (1, 0, 2, 3))
+    back = lax.all_to_all(packed(by_block), "seq", 0, 0, tiled=True)
+    return unpacked(back, pooled_rows, out_width).reshape(batch_count, pooled_rows, out_width)
+
+
+def attention_by_position(pooled, up_weight, norm_gain, qkv_weight, out_weight):
+    batch_count, pooled_rows, channels = pooled.shape
+    group = lax.axis_size(CHANNELS)
+    pooled_all = gathered_packed(pooled, CHANNELS)
+    up_blocks = up_weight.reshape(up_weight.shape[0], group, channels)
+    hidden = jnp.einsum("nbti,oni->bto", pooled_all, up_blocks, precision=MATMUL_PRECISION)
+    hidden_all = gathered_packed(hidden, CHANNELS)
+    positions = (
+        lax.axis_index("seq") * pooled_rows + jnp.arange(pooled_rows, dtype=jnp.int32)
+    ).astype(jnp.float32)
+    query_rows, key_matrix, value_matrix = head_attention(hidden_all, norm_gain, qkv_weight, positions)
+    head_extent = query_rows.shape[-1]
+    keys_and_values = jnp.concatenate([key_matrix, value_matrix], axis=2)
+    kv_all = gathered(keys_and_values, "seq")
+    attention_scores = jnp.einsum(
+        "btc,nbxc->btnx", query_rows, kv_all[..., :head_extent], precision=MATMUL_PRECISION
+    )
+    top = jnp.max(attention_scores, axis=(2, 3))
+    probabilities = jnp.exp(attention_scores - top[..., None, None])
+    denominator = jnp.sum(probabilities, axis=(2, 3))
+    weighted_values = jnp.einsum(
+        "btnx,nbxe->bte", probabilities, kv_all[..., head_extent:], precision=MATMUL_PRECISION
+    )
+    head_result = weighted_values / denominator[..., None]
+    out_width = out_weight.shape[1] // group
+    out_blocks = out_weight.reshape(out_weight.shape[0], group, out_width)
+    shares = jnp.einsum("btd,dne->nbte", head_result, out_blocks, precision=MATMUL_PRECISION)
+    summed = jnp.sum(lax.all_to_all(packed(shares), CHANNELS, 0, 0, tiled=True), axis=0)
+    return unpacked(summed, pooled_rows, out_width)
+
+
 def per_device(
     features,
     first_channel_scale,
@@ -131,41 +232,10 @@
         jnp.max(tower_skip_output.reshape(batch_count, channels, pooled_rows, POOL), axis=3),
         (0, 2, 1),
     )
-    group = lax.axis_size(CHANNELS)
-    pooled_all = gathered(pooled, CHANNELS)
-    up_blocks = up_weight.reshape(up_weight.shape[0], group, channels)
-    hidden = jnp.einsum("nbti,oni->bto", pooled_all, up_blocks, precision=MATMUL_PRECISION)
-    hidden_all = gathered(hidden, CHANNELS)
-    attn_width = norm_gain.shape[0]
-    squares = jnp.sum(hidden_all * hidden_all, axis=(0, 3))
-    gain_blocks = norm_gain.reshape(group, 1, 1, attn_width // group)
-    qkv_blocks = qkv_weight.reshape(group, attn_width // group, qkv_weight.shape[1])
-    projected = jnp.einsum(
-        "nbtj,njo->bto", hidden_all * gain_blocks, qkv_blocks, precision=MATMUL_PRECISION
-    )
-    root_mean = jnp.sqrt(squares / attn_width + 1e-06)
-    projected = projected / root_mean[..., None]
-    head_extent = qkv_weight.shape[1] // 3
-    positions = (
-        lax.axis_index("seq") * pooled_rows + jnp.arange(pooled_rows, dtype=jnp.int32)
-    ).astype(jnp.float32)
-    query_rows = rotate(projected[..., :head_extent], positions) / math.sqrt(head_extent)
-    key_matrix = rotate(projected[..., head_extent : 2 * head_extent], positions)
-    keys_and_values = jnp.concatenate([key_matrix, projected[..., 2 * head_extent :]], axis=2)
-    kv_all = gathered(keys_and_values, "seq")
-    attention_scores = jnp.einsum(
-        "btc,nbxc->btnx", query_rows, kv_all[..., :head_extent], precision=MATMUL_PRECISION
-    )
-    top = jnp.max(attention_scores, axis=(2, 3))
-    probabilities = jnp.exp(attention_scores - top[..., None, None])
-    denominator = jnp.sum(probabilities, axis=(2, 3))
-    weighted_values = jnp.einsum(
-        "btnx,nbxe->bte", probabilities, kv_all[..., head_extent:], precision=MATMUL_PRECISION
-    )
-    head_result = weighted_values / denominator[..., None]
-    out_blocks = out_weight.reshape(out_weight.shape[0], group, out_weight.shape[1] // group)
-    shares = jnp.einsum("btd,dne->nbte", head_result, out_blocks, precision=MATMUL_PRECISION)
-    attended = summed_scatter(shares, CHANNELS)
+    if batch_count % lax.axis_size("seq") == 0:
+        attended = attention_by_batch(pooled, up_weight, norm_gain, qkv_weight, out_weight)
+    else:
+        attended = attention_by_position(pooled, up_weight, norm_gain, qkv_weight, out_weight)
     return (tower_skip_output, attended)
 
 

time: 297 us -> 270 us (0.909)
  waiting for transfers between devices: 102 us -> 40 us
  blocking collectives: 80.2 us -> 113 us
  local copies, waits for them, and re-layouts: 38.7 us -> 44.1 us
  starting transfers between devices: 25.7 us -> 20.4 us
    all_to_all x3 -> x2, waiting for transfers between devices: 68.4 us -> 25.5 us  [gathered(): return lax.all_to_all(copies, axis_name, 0, 0, tiled=True)]
    all_to_all x0 -> x2, blocking collectives: none -> 33.2 us  [the longest x1 24.5 us: attention_by_batch(): lax.all_to_all(packed(shares), CHANNELS, 0, 0, tiled=True)]
    all_to_all x1, waiting for transfers between devices: 25.4 us -> 6.05 us  [attention_by_batch(): back = lax.all_to_all(packed(by_block), 'seq', 0, 0, tiled=True)]
    reshape x2 -> x7, local copies, waits for them, and re-layouts: 2.1 us -> 7.27 us  [the longest x3 3.07 us: packed(): return x.reshape(x.shape[:-2] + (rows * width // LANES, LANES))]
    all_to_all x3 -> x2, starting transfers between devices: 10.9 us -> 7.35 us  [gathered(): return lax.all_to_all(copies, axis_name, 0, 0, tiled=True)]
  transfers between devices with their start and end apart: 10 -> 9, of which waited for: 7 -> 6; matrix products, arithmetic and copies ran while one was open for 8% -> 9% of each run, Pallas kernels for 0% -> 0%
where the time goes in v1:
time: 270 us; the launch traced here: 269 us
  blocking collectives  113 us (42%)
  local copies, waits for them, and re-layouts  44.1 us (16%)
  waiting for transfers between devices  40 us (15%)
  matrix products  34.4 us (13%)
  starting transfers between devices  20.4 us (8%)
  other arithmetic  15.2 us (6%)
    all_to_all x2, blocking collectives, gathered(): return lax.all_to_all(copies, axis_name, 0, 0, tiled=True)  80.2 us
    all_to_all x2, waiting for transfers between devices, gathered(): return lax.all_to_all(copies, axis_name, 0, 0, tiled=True)  25.5 us
    all_to_all x1, blocking collectives, attention_by_batch(): lax.all_to_all(packed(shares), CHANNELS, 0, 0, tiled=True)  24.5 us
    dot_general x2, matrix products, convolution_block(): jnp.einsum('rbit,rio->bot', other_core, other_weights, precision=MATMUL_P...  14.7 us
    reshape x2, local copies, waits for them, and re-layouts, convolution_block(): products = products.reshape(batch_count, tap_count, out_count, rows)  11.1 us
    ppermute x4, starting transfers between devices, shifted_in(): return lax.ppermute(edge, 'seq', pairs)  9.72 us
    dot_general x2, matrix products, convolution_block(): jnp.einsum('rbit,rio->bot', by_row, own_weights, precision=MATMUL_PRECISION)  9.51 us
    all_to_all x1, blocking collectives, attention_by_batch(): lax.all_to_all(pooled.reshape(seq, per, pooled_rows, channels), 'seq', 0,...  8.7 us
  transfers between devices with their start and end apart: 9, of which 6 were waited for; matrix products, arithmetic and copies ran while one was open for 9% of the time, Pallas kernels for 0%

profile of v1, /device:TPU:0, one launch (start us, length us, event | category | flops | bytes accessed | tf_op | source)
XLA Modules:
  0.0 268.6 jit_solution(18224859630137635988)
XLA Ops:
  2.1 3.0 %fusion.23 = f32[8,96,256]{1,2,0:T(8,128)S(1)} fusion(f32[8,96,256]{1,2,0:T(8,128)S(1)} %copy.62, f32[96]{0:T(128)} %param.15, f32[96]{0:T(128)} %param.14), kind=kLoop, calls=%fused_computation.37 | loop fusion | flops 12976128 | bytes 1573632 | tf_op jit(solution)/shard_map/mul | solution.py:41
  5.8 41.6 %all_to_all.35 = f32[4,8,96,256]{3,2,1,0:T(8,128)S(1)} all-to-all(f32[4,8,96,256]{3,2,1,0:T(8,128)S(1)} %broadcast_in_dim.16), channel_id=1, replica_groups=mesh['seq'=4,'crow'=4,'ccol'=2] {'crow'}, dimensions={0} | all-to-all | bytes 6291456 | tf_op jit(solution)/shard_map/all_to_all | solution.py:20
  47.4 1.9 copy.59
  49.3 3.0 %copy.56 = f32[768,480]{1,0:T(8,128)} copy(f32[768,480]{0,1:T(8,128)} %bitcast.127) | data formatting | bytes 2949120 | tf_op jit(solution)/shard_map/transpose | solution.py:48
  52.3 4.8 %fusion.47 = f32[480,8,256,1]{2,0,1,3:T(8,128)S(1)} fusion(f32[4,8,96,256]{3,2,1,0:T(8,128)S(1)} %all_to_all.35, f32[4,2,96,480]{3,2,1,0:T(8,128)} %bitcast.121, s32[]{:T(128)S(6)} %select_n.9), kind=kOutput, calls=%fused_computation.82 | convolution fusion | flops 2264924160 | bytes 7864324 | tf_op jit(solution)/shard_map/rbit,rio->bot/dot_general | solution.py:52
  57.1 7.4 %bitcast_add_fusion.1 = f32[480,8,256]{2,0,1:T(8,128)} fusion(f32[480,8,256,1]{2,0,1,3:T(8,128)S(1)} %fusion.47, f32[4,8,96,256]{3,2,0,1:T(8,128)} %collective-permute-done, f32[4,2,96,480]{3,2,1,0:T(8,128)S(1)} %bitcast.122, s32[]{:T(128)S(6)} %select_n.10), kind=kOutput, calls=%fused_computation.12 | convolution fusion | flops 2265907200 | bytes 11796484 | tf_op jit(solution)/shard_map/rbit,rio->bot/dot_general | solution.py:54
  64.4 5.6 %copy.61 = f32[8,5,96,256]{2,3,0,1:T(8,128)} copy(f32[8,5,96,256]{3,2,1,0:T(8,128)} %bitcast.119) | data formatting | bytes 7864320 | tf_op jit(solution)/shard_map/reshape | solution.py:56
  70.0 3.1 %fusion.21 = f32[8,96,264]{1,2,0:T(8,128)S(1)} fusion(f32[8,5,96,256]{2,3,0,1:T(8,128)} %copy.61), kind=kLoop, calls=%fused_computation.35 | loop fusion | flops 811008 | bytes 4743168 | tf_op jit(solution)/shard_map/add | solution.py:63
  73.1 3.5 %collective-permute-start.1 = (f32[8,4,96]{2,1,0:T(4,128)S(1)}, f32[8,4,96]{2,1,0:T(4,128)S(1)}, u32[]{:S(2)}, u32[]{:S(2)}) collective-permute-start(f32[8,4,96]{2,1,0:T(4,128)S(1)} %get-tuple-element.12), channel_id=1, source_target_pairs={{0,8},{8,16},{16,24},{1,9},{9,17},{17,25},{2,10},{10,18},{18,26},{... | collective-permute-start | bytes 36872 | tf_op jit(solution)/shard_map/ppermute | solution.py:37
  78.2 4.1 %collective-permute-done.2 = f32[8,4,96]{2,1,0:T(4,128)S(1)} collective-permute-done((f32[8,4,96]{2,1,0:T(4,128)S(1)}, f32[8,4,96]{2,1,0:T(4,128)S(1)}, u32[]{:S(2)}, u32[]{:S(2)}) %collective-permute-start.2) | collective-permute-done | bytes 12320 | tf_op jit(solution)/shard_map/ppermute | solution.py:37
  82.3 2.9 %fusion.25 = f32[8,96,256]{1,2,0:T(8,128)S(1)} fusion(f32[96]{0:T(128)S(1)} %copy-done.11, f32[96]{0:T(128)S(1)} %copy-done.12, f32[96]{0:T(128)S(1)} %copy-done.10, f32[8,96,256]{1,2,0:T(8,128)S(1)} %copy-done.1, f32[8,96,4]{1,2,0:T(4,128)S(1)} %bitcast.134, f32[256]{0:T(256)S(1)} %pad.18.clone, f32[8,96,4]{1,2,0:T(4,128)S(1)} %bitcast.132, ...), kind=kLoop, calls=%fused_computation.39 | loop fusion | flops 13959168 | bytes 2386048 | tf_op jit(solution)/shard_map/mul | solution.py:41
  85.9 38.7 %all_to_all.36 = f32[4,8,96,256]{3,2,1,0:T(8,128)S(1)} all-to-all(f32[4,8,96,256]{3,2,1,0:T(8,128)S(1)} %broadcast_in_dim.18), channel_id=1, replica_groups=mesh['seq'=4,'crow'=4,'ccol'=2] {'crow'}, dimensions={0} | all-to-all | bytes 6291456 | tf_op jit(solution)/shard_map/all_to_all | solution.py:20
  124.5 1.9 copy.65
  126.4 3.0 %copy.63 = f32[768,480]{1,0:T(8,128)} copy(f32[768,480]{0,1:T(8,128)} %bitcast.128) | data formatting | bytes 2949120 | tf_op jit(solution)/shard_map/transpose | solution.py:48
  129.4 4.8 %fusion.45 = f32[480,8,256,1]{2,0,1,3:T(8,128)S(1)} fusion(f32[4,8,96,256]{3,2,1,0:T(8,128)S(1)} %all_to_all.36, f32[4,2,96,480]{3,2,1,0:T(8,128)} %bitcast.123, s32[]{:T(128)S(6)} %select_n.9), kind=kOutput, calls=%fused_computation.80 | convolution fusion | flops 2264924160 | bytes 7864324 | tf_op jit(solution)/shard_map/rbit,rio->bot/dot_general | solution.py:52
  134.2 7.4 %bitcast_add_fusion = f32[480,8,256]{2,0,1:T(8,128)} fusion(f32[480,8,256,1]{2,0,1,3:T(8,128)S(1)} %fusion.45, f32[4,8,96,256]{3,2,0,1:T(8,128)} %collective-permute-done.3, f32[4,2,96,480]{3,2,1,0:T(8,128)S(1)} %bitcast.124, s32[]{:T(128)S(6)} %select_n.10), kind=kOutput, calls=%fused_computation.11 | convolution fusion | flops 2265907200 | bytes 11796484 | tf_op jit(solution)/shard_map/rbit,rio->bot/dot_general | solution.py:54
  141.6 5.6 %copy.67 = f32[8,5,96,256]{2,3,0,1:T(8,128)} copy(f32[8,5,96,256]{3,2,1,0:T(8,128)} %bitcast.118) | data formatting | bytes 7864320 | tf_op jit(solution)/shard_map/reshape | solution.py:56
  147.2 3.1 %fusion.16 = f32[8,96,272]{1,2,0:T(8,128)S(1)} fusion(f32[8,5,96,256]{2,3,0,1:T(8,128)} %copy.67), kind=kLoop, calls=%fused_computation.30 | loop fusion | flops 835584 | bytes 4767744 | tf_op jit(solution)/shard_map/add | solution.py:63
  150.3 3.5 %collective-permute-start.4 = (f32[8,8,96]{2,1,0:T(8,128)S(1)}, f32[8,8,96]{2,1,0:T(8,128)S(1)}, u32[]{:S(2)}, u32[]{:S(2)}) collective-permute-start(f32[8,8,96]{2,1,0:T(8,128)S(1)} %get-tuple-element.10), channel_id=1, source_target_pairs={{0,8},{8,16},{16,24},{1,9},{9,17},{17,25},{2,10},{10,18},{18,26},{... | collective-permute-start | bytes 73736 | tf_op jit(solution)/shard_map/ppermute | solution.py:37
  155.3 4.2 %collective-permute-done.5 = f32[8,8,96]{2,1,0:T(8,128)S(1)} collective-permute-done((f32[8,8,96]{2,1,0:T(8,128)S(1)}, f32[8,8,96]{2,1,0:T(8,128)S(1)}, u32[]{:S(2)}, u32[]{:S(2)}) %collective-permute-start.5) | collective-permute-done | bytes 24608 | tf_op jit(solution)/shard_map/ppermute | solution.py:37
  161.2 8.7 %all_to_all.37 = f32[4,2,32,96]{3,2,1,0:T(8,128)S(1)} all-to-all(f32[4,2,32,96]{3,2,1,0:T(8,128)S(1)} %bitcast.130), channel_id=1, replica_groups=mesh['seq'=4,'crow'=4,'ccol'=2] {'seq'}, dimensions={0} | all-to-all | bytes 196608 | tf_op jit(solution)/shard_map/all_to_all | solution.py:137
  171.0 3.8 %all-to-all-start.3 = ((f32[8,2,96,128]{3,2,1,0:T(8,128)}), f32[8,2,96,128]{3,2,1,0:T(8,128)S(1)}, u32[]{:S(2)}, u32[]{:S(2)}) async-start(f32[8,2,96,128]{3,2,1,0:T(8,128)} %broadcast_in_dim.21), calls=%async_computation.3 | async-start | bytes 1572864 | tf_op jit(solution)/shard_map/all_to_all | solution.py:20
  175.2 11.9 %all-to-all-done.3 = f32[8,2,96,128]{3,2,1,0:T(8,128)S(1)} async-done(((f32[8,2,96,128]{3,2,1,0:T(8,128)}), f32[8,2,96,128]{3,2,1,0:T(8,128)S(1)}, u32[]{:S(2)}, u32[]{:S(2)}) %all-to-all-start.3) | async-done | bytes 786464 | tf_op jit(solution)/shard_map/all_to_all | solution.py:20
  189.6 3.6 %all-to-all-start.4 = ((f32[8,2,192,128]{3,2,1,0:T(8,128)}), f32[8,2,192,128]{3,2,1,0:T(8,128)S(1)}, u32[]{:S(2)}, u32[]{:S(2)}) async-start(f32[8,2,192,128]{3,2,1,0:T(8,128)} %broadcast_in_dim.23), calls=%async_computation.4 | async-start | bytes 3145728 | tf_op jit(solution)/shard_map/all_to_all | solution.py:20
  193.2 5.3 %copy.72 = f32[1536,576]{1,0:T(8,128)} copy(f32[1536,576]{0,1:T(8,128)} %param.24) | data formatting | bytes 7077888 | tf_op args[11]
  200.6 13.6 %all-to-all-done.4 = f32[8,2,192,128]{3,2,1,0:T(8,128)S(1)} async-done(((f32[8,2,192,128]{3,2,1,0:T(8,128)}), f32[8,2,192,128]{3,2,1,0:T(8,128)S(1)}, u32[]{:S(2)}, u32[]{:S(2)}) %all-to-all-start.4) | async-done | bytes 1572896 | tf_op jit(solution)/shard_map/all_to_all | solution.py:20
  217.9 6.8 %fusion.6 = f32[2,128,576]{1,2,0:T(8,128)S(1)} fusion(f32[8,192,576,1]{2,1,3,0:T(8,128)} %bitcast.120, f32[8,2,128,192]{3,2,1,0:T(8,128)} %reshape.152, f32[8,192]{1,0:T(8,128)S(1)} %mul.194, f32[2,128]{1,0:T(2,128)S(1)} %add_sqrt_fusion), kind=kOutput, calls=%fused_computation.20 | convolution fusion | flops 1359495168 | bytes 5708800 | tf_op jit(solution)/shard_map/nbtj,njo->bto/dot_general | solution.py:120
  225.6 1.9 convolution_bitcast_fusion
  229.4 2.2 reshape.155
  231.7 24.5 %all_to_all.38 = f32[8,2,192,128]{3,2,1,0:T(8,128)S(1)} all-to-all(f32[8,2,192,128]{3,2,1,0:T(8,128)} %reshape.155), channel_id=1, replica_groups=mesh['seq'=4,'crow'=4,'ccol'=2] {'crow','ccol'}, dimensions={0} | all-to-all | bytes 3145728 | tf_op jit(solution)/shard_map/all_to_all | solution.py:158
  257.2 3.4 %all-to-all-start.6 = ((f32[4,2,48,128]{3,2,1,0:T(8,128)}), f32[4,2,48,128]{3,2,1,0:T(8,128)S(1)}, u32[]{:S(2)}, u32[]{:S(2)}) async-start(f32[4,2,48,128]{3,2,1,0:T(8,128)} %copy.77), calls=%async_computation.6 | async-start | bytes 393216 | tf_op jit(solution)/shard_map/all_to_all | solution.py:161
  261.8 6.0 %all-to-all-done.6 = f32[4,2,48,128]{3,2,1,0:T(8,128)S(1)} async-done(((f32[4,2,48,128]{3,2,1,0:T(8,128)}), f32[4,2,48,128]{3,2,1,0:T(8,128)S(1)}, u32[]{:S(2)}, u32[]{:S(2)}) %all-to-all-start.6) | async-done | bytes 196640 | tf_op jit(solution)/shard_map/all_to_all | solution.py:161
  (77 shorter events, 23.1 us)
Async XLA Ops:
  2.1 3.3 %copy-start = (f32[8,96,256]{1,2,0:T(8,128)}, f32[8,96,256]{1,2,0:T(8,128)S(1)}, u32[]{:S(2)}) copy-start(f32[8,96,256]{1,2,0:T(8,128)S(1)} %copy.62) | copy-start | bytes 2359300
  49.3 7.8 %collective-permute-start = (f32[4,8,96,256]{3,2,0,1:T(8,128)}, f32[4,8,96,256]{3,2,0,1:T(8,128)}, u32[]{:S(2)}, u32[]{:S(2)}) collective-permute-start(f32[4,8,96,256]{3,2,0,1:T(8,128)} %copy.59), channel_id=1, source_target_pairs={{0,1},{1,0},{2,3},{3,2},{4,5},{5,4},{6,7},{7,6},{8,9},{9,8},{10,11... | collective-permute-start | bytes 9437192 | tf_op jit(solution)/shard_map/ppermute | solution.py:28
  52.3 4.8 %copy-start.5 = (f32[768,480]{1,0:T(8,128)S(1)}, f32[768,480]{1,0:T(8,128)}, u32[]{:S(2)}) copy-start(f32[768,480]{1,0:T(8,128)} %copy.56) | copy-start | bytes 4423684
  70.0 12.3 %copy-start.1 = (f32[8,96,256]{1,2,0:T(8,128)S(1)}, f32[8,96,256]{1,2,0:T(8,128)}, u32[]{:S(2)}) copy-start(f32[8,96,256]{1,2,0:T(8,128)} %copy-done) | copy-start | bytes 2359300
  70.0 12.3 %copy-start.10 = (f32[96]{0:T(128)S(1)}, f32[96]{0:T(128)}, u32[]{:S(2)}) copy-start(f32[96]{0:T(128)} %param.16) | copy-start | bytes 1156
  70.0 12.3 %copy-start.11 = (f32[96]{0:T(128)S(1)}, f32[96]{0:T(128)}, u32[]{:S(2)}) copy-start(f32[96]{0:T(128)} %param.19) | copy-start | bytes 1156
  70.0 12.3 %copy-start.12 = (f32[96]{0:T(128)S(1)}, f32[96]{0:T(128)}, u32[]{:S(2)}) copy-start(f32[96]{0:T(128)} %param.18) | copy-start | bytes 1156
  73.1 9.2 %copy-start.3 = (f32[8,96,264]{1,2,0:T(8,128)}, f32[8,96,264]{1,2,0:T(8,128)S(1)}, u32[]{:S(2)}) copy-start(f32[8,96,264]{1,2,0:T(8,128)S(1)} %fusion.21) | copy-start | bytes 2433028
  73.1 5.1 %collective-permute-start.1 = (f32[8,4,96]{2,1,0:T(4,128)S(1)}, f32[8,4,96]{2,1,0:T(4,128)S(1)}, u32[]{:S(2)}, u32[]{:S(2)}) collective-permute-start(f32[8,4,96]{2,1,0:T(4,128)S(1)} %get-tuple-element.12), channel_id=1, source_target_pairs={{0,8},{8,16},{16,24},{1,9},{9,17},{17,25},{2,10},{10,18},{18,26},{... | collective-permute-start | bytes 36872 | tf_op jit(solution)/shard_map/ppermute | solution.py:37
  76.6 5.6 %collective-permute-start.2 = (f32[8,4,96]{2,1,0:T(4,128)S(1)}, f32[8,4,96]{2,1,0:T(4,128)S(1)}, u32[]{:S(2)}, u32[]{:S(2)}) collective-permute-start(f32[8,4,96]{2,1,0:T(4,128)S(1)} %get-tuple-element.13), channel_id=1, source_target_pairs={{8,0},{16,8},{24,16},{9,1},{17,9},{25,17},{10,2},{18,10},{26,18},{... | collective-permute-start | bytes 36872 | tf_op jit(solution)/shard_map/ppermute | solution.py:37
  126.4 7.8 %collective-permute-start.3 = (f32[4,8,96,256]{3,2,0,1:T(8,128)}, f32[4,8,96,256]{3,2,0,1:T(8,128)}, u32[]{:S(2)}, u32[]{:S(2)}) collective-permute-start(f32[4,8,96,256]{3,2,0,1:T(8,128)} %copy.65), channel_id=1, source_target_pairs={{0,1},{1,0},{2,3},{3,2},{4,5},{5,4},{6,7},{7,6},{8,9},{9,8},{10,11... | collective-permute-start | bytes 9437192 | tf_op jit(solution)/shard_map/ppermute | solution.py:28
  129.4 4.8 %copy-start.6 = (f32[768,480]{1,0:T(8,128)S(1)}, f32[768,480]{1,0:T(8,128)}, u32[]{:S(2)}) copy-start(f32[768,480]{1,0:T(8,128)} %copy.63) | copy-start | bytes 4423684
  147.1 12.4 %copy-start.2 = (f32[8,96,256]{1,2,0:T(8,128)S(1)}, f32[8,96,256]{1,2,0:T(8,128)}, u32[]{:S(2)}) copy-start(f32[8,96,256]{1,2,0:T(8,128)} %copy-done) | copy-start | bytes 2359300
  147.1 12.4 %copy-start.4 = (f32[8,96,264]{1,2,0:T(8,128)S(1)}, f32[8,96,264]{1,2,0:T(8,128)}, u32[]{:S(2)}) copy-start(f32[8,96,264]{1,2,0:T(8,128)} %copy-done.3) | copy-start | bytes 2433028
  147.2 12.4 %copy-start.13 = (f32[96]{0:T(128)S(1)}, f32[96]{0:T(128)}, u32[]{:S(2)}) copy-start(f32[96]{0:T(128)} %param.20) | copy-start | bytes 1156
  150.3 5.1 %collective-permute-start.4 = (f32[8,8,96]{2,1,0:T(8,128)S(1)}, f32[8,8,96]{2,1,0:T(8,128)S(1)}, u32[]{:S(2)}, u32[]{:S(2)}) collective-permute-start(f32[8,8,96]{2,1,0:T(8,128)S(1)} %get-tuple-element.10), channel_id=1, source_target_pairs={{0,8},{8,16},{16,24},{1,9},{9,17},{17,25},{2,10},{10,18},{18,26},{... | collective-permute-start | bytes 73736 | tf_op jit(solution)/shard_map/ppermute | solution.py:37
  153.7 5.8 %collective-permute-start.5 = (f32[8,8,96]{2,1,0:T(8,128)S(1)}, f32[8,8,96]{2,1,0:T(8,128)S(1)}, u32[]{:S(2)}, u32[]{:S(2)}) collective-permute-start(f32[8,8,96]{2,1,0:T(8,128)S(1)} %get-tuple-element.11), channel_id=1, source_target_pairs={{8,0},{16,8},{24,16},{9,1},{17,9},{25,17},{10,2},{18,10},{26,18},{... | collective-permute-start | bytes 73736 | tf_op jit(solution)/shard_map/ppermute | solution.py:37
  161.2 13.6 %copy-start.8 = (f32[192,768]{1,0:T(8,128)S(1)}, f32[192,768]{1,0:T(8,128)}, u32[]{:S(2)}) copy-start(f32[192,768]{1,0:T(8,128)} %param.22) | copy-start | bytes 1769476
  171.0 16.1 %all-to-all-start.3 = ((f32[8,2,96,128]{3,2,1,0:T(8,128)}), f32[8,2,96,128]{3,2,1,0:T(8,128)S(1)}, u32[]{:S(2)}, u32[]{:S(2)}) async-start(f32[8,2,96,128]{3,2,1,0:T(8,128)} %broadcast_in_dim.21), calls=%async_computation.3 | async-start | bytes 1572864 | tf_op jit(solution)/shard_map/all_to_all | solution.py:20
  189.6 24.5 %all-to-all-start.4 = ((f32[8,2,192,128]{3,2,1,0:T(8,128)}), f32[8,2,192,128]{3,2,1,0:T(8,128)S(1)}, u32[]{:S(2)}, u32[]{:S(2)}) async-start(f32[8,2,192,128]{3,2,1,0:T(8,128)} %broadcast_in_dim.23), calls=%async_computation.4 | async-start | bytes 3145728 | tf_op jit(solution)/shard_map/all_to_all | solution.py:20
  193.2 5.3 %copy-start.9 = (f32[1536]{0:T(1024)S(1)}, f32[1536]{0:T(1024)}, u32[]{:S(2)}) copy-start(f32[1536]{0:T(1024)} %param.23) | copy-start | bytes 18436
  256.1 4.4 %copy-start.7 = (f32[8,96,256]{1,2,0:T(8,128)S(1)}, f32[8,96,256]{1,2,0:T(8,128)}, u32[]{:S(2)}) copy-start(f32[8,96,256]{1,2,0:T(8,128)} %get-tuple-element.9) | copy-start | bytes 2359300
  257.2 10.6 %all-to-all-start.6 = ((f32[4,2,48,128]{3,2,1,0:T(8,128)}), f32[4,2,48,128]{3,2,1,0:T(8,128)S(1)}, u32[]{:S(2)}, u32[]{:S(2)}) async-start(f32[4,2,48,128]{3,2,1,0:T(8,128)} %copy.77), calls=%async_computation.6 | async-start | bytes 393216 | tf_op jit(solution)/shard_map/all_to_all | solution.py:161

commit v2 on v1

--- a/solution.py
+++ b/solution.py
@@ -37,10 +37,23 @@
     return lax.ppermute(edge, "seq", pairs)
 
 
-def convolution_block(inputs, bn_scale, bn_shift, conv_bias, kernel, dilation):
-    activated = jax.nn.gelu(inputs * bn_scale[:, None] + bn_shift[:, None], approximate=False)
+def activation(inputs, bn_scale, bn_shift):
+    return jax.nn.gelu(inputs * bn_scale[:, None] + bn_shift[:, None], approximate=False)
+
+
+def partner(index, step, count):
+    if count & (count - 1) == 0:
+        return index ^ step
+    return (index + step) % count
+
+
+def channel_blocks(activated):
     by_row = gathered(activated, "crow")
-    other_core = swap_ccol(by_row)
+    return by_row, swap_ccol(by_row)
+
+
+def convolution_rest(inputs, blocks, conv_bias, kernel, dilation):
+    by_row, other_core = blocks
     core = lax.axis_index("ccol")
     tap_count, out_count, in_count = kernel.shape
     row_count = lax.axis_size("crow")
@@ -73,6 +86,36 @@
     return inputs + summed + conv_bias[:, None]
 
 
+def tower(features, first_layer, second_layer, halves):
+    piece = features.shape[0] // halves
+    parts = [features[h * piece : (h + 1) * piece] for h in range(halves)]
+    stages = []
+    for layer_index, layer in enumerate((first_layer, second_layer)):
+        bn_scale, bn_shift, conv_bias, kernel, dilation = layer
+        stages.append(layer)
+    previous = None
+    inputs = list(parts)
+    outputs = [None] * halves
+    pending = {}
+    sequence = [(layer_index, h) for layer_index in range(2) for h in range(halves)]
+    done_blocks = {}
+    for position, (layer_index, h) in enumerate(sequence):
+        bn_scale, bn_shift, conv_bias, kernel, dilation = stages[layer_index]
+        if layer_index == 1:
+            lower = done_blocks.pop((0, h))
+            inputs[h] = convolution_rest(inputs[h], lower, *stages[0][2:])
+        activated = activation(inputs[h], bn_scale, bn_shift)
+        if previous is not None:
+            done_blocks[last_key] = previous
+        blocks = channel_blocks(activated)
+        previous = blocks
+        last_key = (layer_index, h)
+    done_blocks[last_key] = previous
+    for h in range(halves):
+        outputs[h] = convolution_rest(inputs[h], done_blocks.pop((1, h)), *stages[1][2:])
+    return jnp.concatenate(outputs, axis=0)
+
+
 def rotate(values, positions):
     half_width = values.shape[-1] // 2
     frequency = jnp.exp(
@@ -211,21 +254,12 @@
     batch_count = features.shape[0]
     channels = features.shape[1]
     row_count = features.shape[2]
-    first_part = convolution_block(
+    halves = 2 if batch_count % 2 == 0 else 1
+    tower_skip_output = tower(
         features,
-        first_channel_scale,
-        first_channel_shift,
-        first_conv_bias,
-        first_kernel_taps,
-        FIRST_DILATION,
-    )
-    tower_skip_output = convolution_block(
-        first_part,
-        second_channel_scale,
-        second_channel_shift,
-        second_conv_bias,
-        second_kernel_taps,
-        SECOND_DILATION,
+        (first_channel_scale, first_channel_shift, first_conv_bias, first_kernel_taps, FIRST_DILATION),
+        (second_channel_scale, second_channel_shift, second_conv_bias, second_kernel_taps, SECOND_DILATION),
+        halves,
     )
     pooled_rows = row_count // POOL
     pooled = jnp.transpose(

time: 270 us -> 296 us (1.096)
  blocking collectives: 113 us -> 32.9 us
  waiting for transfers between devices: 40 us -> 112 us
  starting transfers between devices: 20.4 us -> 48.9 us
  local copies, waits for them, and re-layouts: 44.1 us -> 51.5 us
    all_to_all x2 -> x0, blocking collectives: 80.2 us -> none  [gathered(): return lax.all_to_all(copies, axis_name, 0, 0, tiled=True)]
    all_to_all x2 -> x6, waiting for transfers between devices: 25.5 us -> 97.5 us  [gathered(): return lax.all_to_all(copies, axis_name, 0, 0, tiled=True)]
    all_to_all x2 -> x6, starting transfers between devices: 7.35 us -> 23 us  [gathered(): return lax.all_to_all(copies, axis_name, 0, 0, tiled=True)]
    ppermute x4 -> x8, starting transfers between devices: 9.72 us -> 22.6 us  [shifted_in(): return lax.ppermute(edge, 'seq', pairs)]
    broadcast_in_dim x6 -> x8, local copies, waits for them, and re-layouts: 3.22 us -> 7.81 us  [gathered(): copies = jnp.broadcast_to(x[None], (count,) + x.shape)]
    unnamed x31 -> x76, local copies, waits for them, and re-layouts: 8.02 us -> 9.85 us
    transpose x4 -> x6, local copies, waits for them, and re-layouts: 6.01 us -> 4.9 us  [the longest x2 3.67 us: convolution_rest(): weights = jnp.transpose(kernel.reshape(tap_count * out_count, in_count))]
    dot_general x4 -> x8, matrix products: 24.2 us -> 25.2 us  [the longest x4 18 us: convolution_rest(): jnp.einsum('rbit,rio->bot', other_core, other_weights, precision=MATMUL_P...]
  transfers between devices with their start and end apart: 9 -> 19, of which waited for: 6 -> 9; matrix products, arithmetic and copies ran while one was open for 9% -> 20% of each run, Pallas kernels for 0% -> 0%
where the time goes in v2:
time: 296 us; the launch traced here: 295 us
  waiting for transfers between devices  112 us (38%)
  local copies, waits for them, and re-layouts  51.5 us (17%)
  starting transfers between devices  48.9 us (17%)
  matrix products  35.3 us (12%)
  blocking collectives  32.9 us (11%)
  other arithmetic  12.4 us (4%)
    all_to_all x6, waiting for transfers between devices, gathered(): return lax.all_to_all(copies, axis_name, 0, 0, tiled=True)  97.5 us
    all_to_all x1, blocking collectives, attention_by_batch(): lax.all_to_all(packed(shares), CHANNELS, 0, 0, tiled=True)  24.5 us
    all_to_all x6, starting transfers between devices, gathered(): return lax.all_to_all(copies, axis_name, 0, 0, tiled=True)  23 us
    ppermute x8, starting transfers between devices, shifted_in(): return lax.ppermute(edge, 'seq', pairs)  22.6 us
    dot_general x4, matrix products, convolution_rest(): jnp.einsum('rbit,rio->bot', other_core, other_weights, precision=MATMUL_P...  18 us
    reshape x4, local copies, waits for them, and re-layouts, convolution_rest(): products = products.reshape(batch_count, tap_count, out_count, rows)  10.2 us
    unnamed x76, local copies, waits for them, and re-layouts  9.85 us
    all_to_all x1, blocking collectives, attention_by_batch(): lax.all_to_all(pooled.reshape(seq, per, pooled_rows, channels), 'seq', 0,...  8.44 us
  transfers between devices with their start and end apart: 19, of which 9 were waited for; matrix products, arithmetic and copies ran while one was open for 20% of the time, Pallas kernels for 0%

profile of v2, /device:TPU:0, one launch (start us, length us, event | category | flops | bytes accessed | tf_op | source)
XLA Modules:
  0.0 294.5 jit_solution(11494926965333632389)
XLA Ops:
  2.3 2.3 fusion.55
  6.1 5.2 %all-to-all-start.2 = ((f32[4,4,96,256]{3,2,1,0:T(8,128)}), f32[4,4,96,256]{3,2,1,0:T(8,128)S(1)}, u32[]{:S(2)}, u32[]{:S(2)}) async-start(f32[4,4,96,256]{3,2,1,0:T(8,128)} %broadcast_in_dim.18), calls=%async_computation.2 | async-start | bytes 3145728 | tf_op jit(solution)/shard_map/all_to_all | solution.py:20
  11.5 19.1 %all-to-all-done.2 = f32[4,4,96,256]{3,2,1,0:T(8,128)S(1)} async-done(((f32[4,4,96,256]{3,2,1,0:T(8,128)}), f32[4,4,96,256]{3,2,1,0:T(8,128)S(1)}, u32[]{:S(2)}, u32[]{:S(2)}) %all-to-all-start.2) | async-done | bytes 1572896 | tf_op jit(solution)/shard_map/all_to_all | solution.py:20
  31.8 3.6 %all-to-all-start = ((f32[4,4,96,256]{3,2,1,0:T(8,128)}), f32[4,4,96,256]{3,2,1,0:T(8,128)S(1)}, u32[]{:S(2)}, u32[]{:S(2)}) async-start(f32[4,4,96,256]{3,2,1,0:T(8,128)} %broadcast_in_dim.16), calls=%async_computation | async-start | bytes 3145728 | tf_op jit(solution)/shard_map/all_to_all | solution.py:20
  36.7 17.4 %all-to-all-done = f32[4,4,96,256]{3,2,1,0:T(8,128)S(1)} async-done(((f32[4,4,96,256]{3,2,1,0:T(8,128)}), f32[4,4,96,256]{3,2,1,0:T(8,128)S(1)}, u32[]{:S(2)}, u32[]{:S(2)}) %all-to-all-start) | async-done | bytes 1572896 | tf_op jit(solution)/shard_map/all_to_all | solution.py:20
  61.2 4.5 %bitcast_add_fusion.1 = f32[480,4,256]{2,0,1:T(8,128)} fusion(f32[480,4,256,1]{2,0,1,3:T(8,128)S(1)} %fusion.17, f32[4,4,96,256]{3,2,0,1:T(8,128)} %collective-permute-done.6, f32[4,2,96,480]{3,2,1,0:T(8,128)S(1)} %bitcast.173, s32[]{:T(128)S(6)} %select_n.14), kind=kOutput, calls=%fused_computation.24 | convolution fusion | flops 1132953600 | bytes 6291460 | tf_op jit(solution)/shard_map/rbit,rio->bot/dot_general | solution.py:67
  65.7 3.1 %copy.81 = f32[4,5,96,256]{2,3,0,1:T(8,128)} copy(f32[4,5,96,256]{3,2,1,0:T(8,128)} %bitcast.181) | data formatting | bytes 3932160 | tf_op jit(solution)/shard_map/reshape | solution.py:69
  72.2 3.6 %collective-permute-start.7 = (f32[4,4,96]{2,1,0:T(4,128)}, f32[4,4,96]{2,1,0:T(4,128)S(1)}, u32[]{:S(2)}, u32[]{:S(2)}) collective-permute-start(f32[4,4,96]{2,1,0:T(4,128)} %get-tuple-element.20), channel_id=1, source_target_pairs={{0,8},{8,16},{16,24},{1,9},{9,17},{17,25},{2,10},{10,18},{18,26},{... | collective-permute-start | bytes 18440 | tf_op jit(solution)/shard_map/ppermute | solution.py:37
  77.3 4.5 %bitcast_add_fusion.3 = f32[480,4,256]{2,0,1:T(8,128)} fusion(f32[480,4,256,1]{2,0,1,3:T(8,128)S(1)} %fusion.19, f32[4,4,96,256]{3,2,0,1:T(8,128)} %collective-permute-done, f32[4,2,96,480]{3,2,1,0:T(8,128)S(1)} %bitcast.174, s32[]{:T(128)S(6)} %select_n.14), kind=kOutput, calls=%fused_computation.26 | convolution fusion | flops 1132953600 | bytes 6291460 | tf_op jit(solution)/shard_map/rbit,rio->bot/dot_general | solution.py:67
  84.1 4.7 %collective-permute-start.1 = (f32[4,4,96]{2,1,0:T(4,128)S(1)}, f32[4,4,96]{2,1,0:T(4,128)S(1)}, u32[]{:S(2)}, u32[]{:S(2)}) collective-permute-start(f32[4,4,96]{2,1,0:T(4,128)S(1)} %get-tuple-element.18), channel_id=1, source_target_pairs={{0,8},{8,16},{16,24},{1,9},{9,17},{17,25},{2,10},{10,18},{18,26},{... | collective-permute-start | bytes 18440 | tf_op jit(solution)/shard_map/ppermute | solution.py:37
  90.2 4.1 %collective-permute-done.2 = f32[4,4,96]{2,1,0:T(4,128)S(1)} collective-permute-done((f32[4,4,96]{2,1,0:T(4,128)S(1)}, f32[4,4,96]{2,1,0:T(4,128)S(1)}, u32[]{:S(2)}, u32[]{:S(2)}) %collective-permute-start.2) | collective-permute-done | bytes 6176 | tf_op jit(solution)/shard_map/ppermute | solution.py:37
  94.4 2.9 fusion.57
  98.9 3.6 %all-to-all-start.3 = ((f32[4,4,96,256]{3,2,1,0:T(8,128)}), f32[4,4,96,256]{3,2,1,0:T(8,128)S(1)}, u32[]{:S(2)}, u32[]{:S(2)}) async-start(f32[4,4,96,256]{3,2,1,0:T(8,128)} %broadcast_in_dim.19), calls=%async_computation.3 | async-start | bytes 3145728 | tf_op jit(solution)/shard_map/all_to_all | solution.py:20
  102.6 18.0 %all-to-all-done.3 = f32[4,4,96,256]{3,2,1,0:T(8,128)S(1)} async-done(((f32[4,4,96,256]{3,2,1,0:T(8,128)}), f32[4,4,96,256]{3,2,1,0:T(8,128)S(1)}, u32[]{:S(2)}, u32[]{:S(2)}) %all-to-all-start.3) | async-done | bytes 1572896 | tf_op jit(solution)/shard_map/all_to_all | solution.py:20
  121.9 3.6 %all-to-all-start.1 = ((f32[4,4,96,256]{3,2,1,0:T(8,128)}), f32[4,4,96,256]{3,2,1,0:T(8,128)S(1)}, u32[]{:S(2)}, u32[]{:S(2)}) async-start(f32[4,4,96,256]{3,2,1,0:T(8,128)} %broadcast_in_dim.17), calls=%async_computation.1 | async-start | bytes 3145728 | tf_op jit(solution)/shard_map/all_to_all | solution.py:20
  126.8 17.4 %all-to-all-done.1 = f32[4,4,96,256]{3,2,1,0:T(8,128)S(1)} async-done(((f32[4,4,96,256]{3,2,1,0:T(8,128)}), f32[4,4,96,256]{3,2,1,0:T(8,128)S(1)}, u32[]{:S(2)}, u32[]{:S(2)}) %all-to-all-start.1) | async-done | bytes 1572896 | tf_op jit(solution)/shard_map/all_to_all | solution.py:20
  151.3 4.5 %bitcast_add_fusion = f32[480,4,256]{2,0,1:T(8,128)} fusion(f32[480,4,256,1]{2,0,1,3:T(8,128)S(1)} %fusion.13, f32[4,4,96,256]{3,2,0,1:T(8,128)} %collective-permute-done.9, f32[4,2,96,480]{3,2,1,0:T(8,128)S(1)} %bitcast.177, s32[]{:T(128)S(6)} %select_n.14), kind=kOutput, calls=%fused_computation.23 | convolution fusion | flops 1132953600 | bytes 6291460 | tf_op jit(solution)/shard_map/rbit,rio->bot/dot_general | solution.py:67
  155.8 3.1 %copy.85 = f32[4,5,96,256]{2,3,0,1:T(8,128)} copy(f32[4,5,96,256]{3,2,1,0:T(8,128)} %bitcast.182) | data formatting | bytes 3932160 | tf_op jit(solution)/shard_map/reshape | solution.py:69
  162.2 4.1 %collective-permute-start.10 = (f32[4,8,96]{2,1,0:T(8,128)}, f32[4,8,96]{2,1,0:T(8,128)}, u32[]{:S(2)}, u32[]{:S(2)}) collective-permute-start(f32[4,8,96]{2,1,0:T(8,128)} %get-tuple-element.16), channel_id=1, source_target_pairs={{0,8},{8,16},{16,24},{1,9},{9,17},{17,25},{2,10},{10,18},{18,26},{... | collective-permute-start | bytes 36872 | tf_op jit(solution)/shard_map/ppermute | solution.py:37
  167.8 4.5 %bitcast_add_fusion.2 = f32[480,4,256]{2,0,1:T(8,128)} fusion(f32[480,4,256,1]{2,0,1,3:T(8,128)S(1)} %fusion.15, f32[4,4,96,256]{3,2,0,1:T(8,128)} %collective-permute-done.3, f32[4,2,96,480]{3,2,1,0:T(8,128)S(1)} %bitcast.178, s32[]{:T(128)S(6)} %select_n.14), kind=kOutput, calls=%fused_computation.25 | convolution fusion | flops 1132953600 | bytes 6291460 | tf_op jit(solution)/shard_map/rbit,rio->bot/dot_general | solution.py:67
  174.7 4.7 %collective-permute-start.4 = (f32[4,8,96]{2,1,0:T(8,128)S(1)}, f32[4,8,96]{2,1,0:T(8,128)S(1)}, u32[]{:S(2)}, u32[]{:S(2)}) collective-permute-start(f32[4,8,96]{2,1,0:T(8,128)S(1)} %get-tuple-element.14), channel_id=1, source_target_pairs={{0,8},{8,16},{16,24},{1,9},{9,17},{17,25},{2,10},{10,18},{18,26},{... | collective-permute-start | bytes 36872 | tf_op jit(solution)/shard_map/ppermute | solution.py:37
  180.8 4.2 %collective-permute-done.5 = f32[4,8,96]{2,1,0:T(8,128)S(1)} collective-permute-done((f32[4,8,96]{2,1,0:T(8,128)S(1)}, f32[4,8,96]{2,1,0:T(8,128)S(1)}, u32[]{:S(2)}, u32[]{:S(2)}) %collective-permute-start.5) | collective-permute-done | bytes 12320 | tf_op jit(solution)/shard_map/ppermute | solution.py:37
  187.3 8.4 %all_to_all.45 = f32[4,2,32,96]{3,2,1,0:T(8,128)S(1)} all-to-all(f32[4,2,32,96]{3,2,1,0:T(8,128)S(1)} %bitcast.188), channel_id=1, replica_groups=mesh['seq'=4,'crow'=4,'ccol'=2] {'seq'}, dimensions={0} | all-to-all | bytes 196608 | tf_op jit(solution)/shard_map/all_to_all | solution.py:180
  196.8 3.5 %all-to-all-start.5 = ((f32[8,2,96,128]{3,2,1,0:T(8,128)}), f32[8,2,96,128]{3,2,1,0:T(8,128)S(1)}, u32[]{:S(2)}, u32[]{:S(2)}) async-start(f32[8,2,96,128]{3,2,1,0:T(8,128)} %broadcast_in_dim.21), calls=%async_computation.5 | async-start | bytes 1572864 | tf_op jit(solution)/shard_map/all_to_all | solution.py:20
  200.8 12.1 %all-to-all-done.5 = f32[8,2,96,128]{3,2,1,0:T(8,128)S(1)} async-done(((f32[8,2,96,128]{3,2,1,0:T(8,128)}), f32[8,2,96,128]{3,2,1,0:T(8,128)S(1)}, u32[]{:S(2)}, u32[]{:S(2)}) %all-to-all-start.5) | async-done | bytes 786464 | tf_op jit(solution)/shard_map/all_to_all | solution.py:20
  215.4 3.6 %all-to-all-start.6 = ((f32[8,2,192,128]{3,2,1,0:T(8,128)}), f32[8,2,192,128]{3,2,1,0:T(8,128)S(1)}, u32[]{:S(2)}, u32[]{:S(2)}) async-start(f32[8,2,192,128]{3,2,1,0:T(8,128)} %broadcast_in_dim.23), calls=%async_computation.6 | async-start | bytes 3145728 | tf_op jit(solution)/shard_map/all_to_all | solution.py:20
  219.0 5.3 %copy.90 = f32[1536,576]{1,0:T(8,128)} copy(f32[1536,576]{0,1:T(8,128)} %param.24) | data formatting | bytes 7077888 | tf_op args[11]
  226.4 13.5 %all-to-all-done.6 = f32[8,2,192,128]{3,2,1,0:T(8,128)S(1)} async-done(((f32[8,2,192,128]{3,2,1,0:T(8,128)}), f32[8,2,192,128]{3,2,1,0:T(8,128)S(1)}, u32[]{:S(2)}, u32[]{:S(2)}) %all-to-all-start.6) | async-done | bytes 1572896 | tf_op jit(solution)/shard_map/all_to_all | solution.py:20
  243.8 6.8 %fusion.6 = f32[2,128,576]{1,2,0:T(8,128)S(1)} fusion(f32[8,192,576,1]{2,1,3,0:T(8,128)} %bitcast.170, f32[8,2,128,192]{3,2,1,0:T(8,128)} %reshape.174, f32[8,192]{1,0:T(8,128)S(1)} %mul.232, f32[2,128]{1,0:T(2,128)S(1)} %add_sqrt_fusion), kind=kOutput, calls=%fused_computation.30 | convolution fusion | flops 1359495168 | bytes 5708800 | tf_op jit(solution)/shard_map/nbtj,njo->bto/dot_general | solution.py:163
  257.6 24.5 %all_to_all.46 = f32[8,2,192,128]{3,2,1,0:T(8,128)S(1)} all-to-all(f32[8,2,192,128]{3,2,1,0:T(8,128)} %reshape.177), channel_id=1, replica_groups=mesh['seq'=4,'crow'=4,'ccol'=2] {'crow','ccol'}, dimensions={0} | all-to-all | bytes 3145728 | tf_op jit(solution)/shard_map/all_to_all | solution.py:201
  283.1 3.4 %all-to-all-start.8 = ((f32[4,2,48,128]{3,2,1,0:T(8,128)}), f32[4,2,48,128]{3,2,1,0:T(8,128)S(1)}, u32[]{:S(2)}, u32[]{:S(2)}) async-start(f32[4,2,48,128]{3,2,1,0:T(8,128)} %copy.95), calls=%async_computation.8 | async-start | bytes 393216 | tf_op jit(solution)/shard_map/all_to_all | solution.py:204
  287.7 6.0 %all-to-all-done.8 = f32[4,2,48,128]{3,2,1,0:T(8,128)S(1)} async-done(((f32[4,2,48,128]{3,2,1,0:T(8,128)}), f32[4,2,48,128]{3,2,1,0:T(8,128)S(1)}, u32[]{:S(2)}, u32[]{:S(2)}) %all-to-all-start.8) | async-done | bytes 196640 | tf_op jit(solution)/shard_map/all_to_all | solution.py:204
  (159 shorter events, 63.5 us)
Async XLA Ops:
  6.1 24.4 %all-to-all-start.2 = ((f32[4,4,96,256]{3,2,1,0:T(8,128)}), f32[4,4,96,256]{3,2,1,0:T(8,128)S(1)}, u32[]{:S(2)}, u32[]{:S(2)}) async-start(f32[4,4,96,256]{3,2,1,0:T(8,128)} %broadcast_in_dim.18), calls=%async_computation.2 | async-start | bytes 3145728 | tf_op jit(solution)/shard_map/all_to_all | solution.py:20
  31.8 22.3 %all-to-all-start = ((f32[4,4,96,256]{3,2,1,0:T(8,128)}), f32[4,4,96,256]{3,2,1,0:T(8,128)S(1)}, u32[]{:S(2)}, u32[]{:S(2)}) async-start(f32[4,4,96,256]{3,2,1,0:T(8,128)} %broadcast_in_dim.16), calls=%async_computation | async-start | bytes 3145728 | tf_op jit(solution)/shard_map/all_to_all | solution.py:20
  36.7 24.5 %collective-permute-start.6 = (f32[4,4,96,256]{3,2,0,1:T(8,128)}, f32[4,4,96,256]{3,2,0,1:T(8,128)}, u32[]{:S(2)}, u32[]{:S(2)}) collective-permute-start(f32[4,4,96,256]{3,2,0,1:T(8,128)} %copy.79), channel_id=1, source_target_pairs={{0,1},{1,0},{2,3},{3,2},{4,5},{5,4},{6,7},{7,6},{8,9},{9,8},{10,11... | collective-permute-start | bytes 4718600 | tf_op jit(solution)/shard_map/ppermute | solution.py:28
  55.7 21.5 %collective-permute-start = (f32[4,4,96,256]{3,2,0,1:T(8,128)}, f32[4,4,96,256]{3,2,0,1:T(8,128)}, u32[]{:S(2)}, u32[]{:S(2)}) collective-permute-start(f32[4,4,96,256]{3,2,0,1:T(8,128)} %copy.69), channel_id=1, source_target_pairs={{0,1},{1,0},{2,3},{3,2},{4,5},{5,4},{6,7},{7,6},{8,9},{9,8},{10,11... | collective-permute-start | bytes 4718600 | tf_op jit(solution)/shard_map/ppermute | solution.py:28
  72.2 18.0 %collective-permute-start.7 = (f32[4,4,96]{2,1,0:T(4,128)}, f32[4,4,96]{2,1,0:T(4,128)S(1)}, u32[]{:S(2)}, u32[]{:S(2)}) collective-permute-start(f32[4,4,96]{2,1,0:T(4,128)} %get-tuple-element.20), channel_id=1, source_target_pairs={{0,8},{8,16},{16,24},{1,9},{9,17},{17,25},{2,10},{10,18},{18,26},{... | collective-permute-start | bytes 18440 | tf_op jit(solution)/shard_map/ppermute | solution.py:37
  75.8 14.4 %collective-permute-start.8 = (f32[4,4,96]{2,1,0:T(4,128)}, f32[4,4,96]{2,1,0:T(4,128)S(1)}, u32[]{:S(2)}, u32[]{:S(2)}) collective-permute-start(f32[4,4,96]{2,1,0:T(4,128)} %get-tuple-element.21), channel_id=1, source_target_pairs={{8,0},{16,8},{24,16},{9,1},{17,9},{25,17},{10,2},{18,10},{26,18},{... | collective-permute-start | bytes 18440 | tf_op jit(solution)/shard_map/ppermute | solution.py:37
  83.8 10.6 %copy-start.5 = (f32[4,96,256]{1,2,0:T(8,128)S(1)}, f32[4,96,256]{1,2,0:T(8,128)}, u32[]{:S(2)}) copy-start(f32[4,96,256]{1,2,0:T(8,128)} %copy-done.4) | copy-start | bytes 1179652
  84.1 13.2 %copy-start.13 = (f32[4,96,264]{1,2,0:T(8,128)}, f32[4,96,264]{1,2,0:T(8,128)S(1)}, u32[]{:S(2)}) copy-start(f32[4,96,264]{1,2,0:T(8,128)S(1)} %fusion.48) | copy-start | bytes 1216516
  84.1 6.1 %collective-permute-start.1 = (f32[4,4,96]{2,1,0:T(4,128)S(1)}, f32[4,4,96]{2,1,0:T(4,128)S(1)}, u32[]{:S(2)}, u32[]{:S(2)}) collective-permute-start(f32[4,4,96]{2,1,0:T(4,128)S(1)} %get-tuple-element.18), channel_id=1, source_target_pairs={{0,8},{8,16},{16,24},{1,9},{9,17},{17,25},{2,10},{10,18},{18,26},{... | collective-permute-start | bytes 18440 | tf_op jit(solution)/shard_map/ppermute | solution.py:37
  88.8 5.5 %collective-permute-start.2 = (f32[4,4,96]{2,1,0:T(4,128)S(1)}, f32[4,4,96]{2,1,0:T(4,128)S(1)}, u32[]{:S(2)}, u32[]{:S(2)}) collective-permute-start(f32[4,4,96]{2,1,0:T(4,128)S(1)} %get-tuple-element.19), channel_id=1, source_target_pairs={{8,0},{16,8},{24,16},{9,1},{17,9},{25,17},{10,2},{18,10},{26,18},{... | collective-permute-start | bytes 18440 | tf_op jit(solution)/shard_map/ppermute | solution.py:37
  98.9 21.7 %all-to-all-start.3 = ((f32[4,4,96,256]{3,2,1,0:T(8,128)}), f32[4,4,96,256]{3,2,1,0:T(8,128)S(1)}, u32[]{:S(2)}, u32[]{:S(2)}) async-start(f32[4,4,96,256]{3,2,1,0:T(8,128)} %broadcast_in_dim.19), calls=%async_computation.3 | async-start | bytes 3145728 | tf_op jit(solution)/shard_map/all_to_all | solution.py:20
  121.9 22.2 %all-to-all-start.1 = ((f32[4,4,96,256]{3,2,1,0:T(8,128)}), f32[4,4,96,256]{3,2,1,0:T(8,128)S(1)}, u32[]{:S(2)}, u32[]{:S(2)}) async-start(f32[4,4,96,256]{3,2,1,0:T(8,128)} %broadcast_in_dim.17), calls=%async_computation.1 | async-start | bytes 3145728 | tf_op jit(solution)/shard_map/all_to_all | solution.py:20
  126.8 24.5 %collective-permute-start.9 = (f32[4,4,96,256]{3,2,0,1:T(8,128)}, f32[4,4,96,256]{3,2,0,1:T(8,128)}, u32[]{:S(2)}, u32[]{:S(2)}) collective-permute-start(f32[4,4,96,256]{3,2,0,1:T(8,128)} %copy.83), channel_id=1, source_target_pairs={{0,1},{1,0},{2,3},{3,2},{4,5},{5,4},{6,7},{7,6},{8,9},{9,8},{10,11... | collective-permute-start | bytes 4718600 | tf_op jit(solution)/shard_map/ppermute | solution.py:28
  145.8 22.0 %collective-permute-start.3 = (f32[4,4,96,256]{3,2,0,1:T(8,128)}, f32[4,4,96,256]{3,2,0,1:T(8,128)}, u32[]{:S(2)}, u32[]{:S(2)}) collective-permute-start(f32[4,4,96,256]{3,2,0,1:T(8,128)} %copy.74), channel_id=1, source_target_pairs={{0,1},{1,0},{2,3},{3,2},{4,5},{5,4},{6,7},{7,6},{8,9},{9,8},{10,11... | collective-permute-start | bytes 4718600 | tf_op jit(solution)/shard_map/ppermute | solution.py:28
  162.2 18.5 %collective-permute-start.10 = (f32[4,8,96]{2,1,0:T(8,128)}, f32[4,8,96]{2,1,0:T(8,128)}, u32[]{:S(2)}, u32[]{:S(2)}) collective-permute-start(f32[4,8,96]{2,1,0:T(8,128)} %get-tuple-element.16), channel_id=1, source_target_pairs={{0,8},{8,16},{16,24},{1,9},{9,17},{17,25},{2,10},{10,18},{18,26},{... | collective-permute-start | bytes 36872 | tf_op jit(solution)/shard_map/ppermute | solution.py:37
  166.3 14.5 %collective-permute-start.11 = (f32[4,8,96]{2,1,0:T(8,128)}, f32[4,8,96]{2,1,0:T(8,128)}, u32[]{:S(2)}, u32[]{:S(2)}) collective-permute-start(f32[4,8,96]{2,1,0:T(8,128)} %get-tuple-element.17), channel_id=1, source_target_pairs={{8,0},{16,8},{24,16},{9,1},{17,9},{25,17},{10,2},{18,10},{26,18},{... | collective-permute-start | bytes 36872 | tf_op jit(solution)/shard_map/ppermute | solution.py:37
  174.3 10.7 %copy-start.6 = (f32[4,96,256]{1,2,0:T(8,128)S(1)}, f32[4,96,256]{1,2,0:T(8,128)}, u32[]{:S(2)}) copy-start(f32[4,96,256]{1,2,0:T(8,128)} %copy-done.4) | copy-start | bytes 1179652
  174.3 10.7 %copy-start.9 = (f32[4,96,256]{1,2,0:T(8,128)S(1)}, f32[4,96,256]{1,2,0:T(8,128)}, u32[]{:S(2)}) copy-start(f32[4,96,256]{1,2,0:T(8,128)} %copy-done.7) | copy-start | bytes 1179652
  174.3 10.7 %copy-start.12 = (f32[4,96,264]{1,2,0:T(8,128)S(1)}, f32[4,96,264]{1,2,0:T(8,128)}, u32[]{:S(2)}) copy-start(f32[4,96,264]{1,2,0:T(8,128)} %copy-done.10) | copy-start | bytes 1216516
  174.3 10.7 %copy-start.14 = (f32[4,96,264]{1,2,0:T(8,128)S(1)}, f32[4,96,264]{1,2,0:T(8,128)}, u32[]{:S(2)}) copy-start(f32[4,96,264]{1,2,0:T(8,128)} %copy-done.13) | copy-start | bytes 1216516
  174.3 10.7 %copy-start.20 = (f32[4,96,272]{1,2,0:T(8,128)S(1)}, f32[4,96,272]{1,2,0:T(8,128)}, u32[]{:S(2)}) copy-start(f32[4,96,272]{1,2,0:T(8,128)} %copy-done.19) | copy-start | bytes 1253380
  174.4 10.7 %copy-start.23 = (f32[4,4,96]{2,1,0:T(4,128)S(1)}, f32[4,4,96]{2,1,0:T(4,128)}, u32[]{:S(2)}) copy-start(f32[4,4,96]{2,1,0:T(4,128)} %copy-done.22) | copy-start | bytes 18436
  174.4 10.7 %copy-start.25 = (f32[4,4,96]{2,1,0:T(4,128)S(1)}, f32[4,4,96]{2,1,0:T(4,128)}, u32[]{:S(2)}) copy-start(f32[4,4,96]{2,1,0:T(4,128)} %copy-done.24) | copy-start | bytes 18436
  174.4 10.7 %copy-start.27 = (f32[256]{0:T(256)S(1)}, f32[256]{0:T(256)}, u32[]{:S(2)}) copy-start(f32[256]{0:T(256)} %copy-done.26) | copy-start | bytes 3076
  174.4 10.7 %copy-start.30 = (f32[96]{0:T(128)S(1)}, f32[96]{0:T(128)}, u32[]{:S(2)}) copy-start(f32[96]{0:T(128)} %param.16) | copy-start | bytes 1156
  174.4 10.7 %copy-start.33 = (f32[96]{0:T(128)S(1)}, f32[96]{0:T(128)}, u32[]{:S(2)}) copy-start(f32[96]{0:T(128)} %param.20) | copy-start | bytes 1156
  174.7 6.1 %collective-permute-start.4 = (f32[4,8,96]{2,1,0:T(8,128)S(1)}, f32[4,8,96]{2,1,0:T(8,128)S(1)}, u32[]{:S(2)}, u32[]{:S(2)}) collective-permute-start(f32[4,8,96]{2,1,0:T(8,128)S(1)} %get-tuple-element.14), channel_id=1, source_target_pairs={{0,8},{8,16},{16,24},{1,9},{9,17},{17,25},{2,10},{10,18},{18,26},{... | collective-permute-start | bytes 36872 | tf_op jit(solution)/shard_map/ppermute | solution.py:37
  179.3 5.6 %collective-permute-start.5 = (f32[4,8,96]{2,1,0:T(8,128)S(1)}, f32[4,8,96]{2,1,0:T(8,128)S(1)}, u32[]{:S(2)}, u32[]{:S(2)}) collective-permute-start(f32[4,8,96]{2,1,0:T(8,128)S(1)} %get-tuple-element.15), channel_id=1, source_target_pairs={{8,0},{16,8},{24,16},{9,1},{17,9},{25,17},{10,2},{18,10},{26,18},{... | collective-permute-start | bytes 36872 | tf_op jit(solution)/shard_map/ppermute | solution.py:37
  187.3 13.1 %copy-start.21 = (f32[192,768]{1,0:T(8,128)S(1)}, f32[192,768]{1,0:T(8,128)}, u32[]{:S(2)}) copy-start(f32[192,768]{1,0:T(8,128)} %param.22) | copy-start | bytes 1769476
  196.8 16.1 %all-to-all-start.5 = ((f32[8,2,96,128]{3,2,1,0:T(8,128)}), f32[8,2,96,128]{3,2,1,0:T(8,128)S(1)}, u32[]{:S(2)}, u32[]{:S(2)}) async-start(f32[8,2,96,128]{3,2,1,0:T(8,128)} %broadcast_in_dim.21), calls=%async_computation.5 | async-start | bytes 1572864 | tf_op jit(solution)/shard_map/all_to_all | solution.py:20
  215.4 24.5 %all-to-all-start.6 = ((f32[8,2,192,128]{3,2,1,0:T(8,128)}), f32[8,2,192,128]{3,2,1,0:T(8,128)S(1)}, u32[]{:S(2)}, u32[]{:S(2)}) async-start(f32[8,2,192,128]{3,2,1,0:T(8,128)} %broadcast_in_dim.23), calls=%async_computation.6 | async-start | bytes 3145728 | tf_op jit(solution)/shard_map/all_to_all | solution.py:20
  283.1 10.6 %all-to-all-start.8 = ((f32[4,2,48,128]{3,2,1,0:T(8,128)}), f32[4,2,48,128]{3,2,1,0:T(8,128)S(1)}, u32[]{:S(2)}, u32[]{:S(2)}) async-start(f32[4,2,48,128]{3,2,1,0:T(8,128)} %copy.95), calls=%async_computation.8 | async-start | bytes 393216 | tf_op jit(solution)/shard_map/all_to_all | solution.py:204
  (23 other events, 104.4 us)
